TPU v7x, 128 devices: a whole 4x4x4 slice. The times are simulated.
128 devices in a mesh: row: 8 (over x, y_lo), col: 16 (over y_hi, z, core).
Axes of the slice: x: 4, y: 4 (y_hi: 2, y_lo: 2; y = y_hi * 2 + y_lo), z: 4, core: 2. Of those that a mesh axis runs over, the one named last changes fastest.
Arguments:
- eigvecs: float32 [2048, 131072], P('col', 'row'), may hold values from -6 to 6
- basis: float32 [2, 131072, 256], P(None, 'row', 'col'), may hold values from -0.0625 to 0.0625
- coupling: float32 [2, 256, 256], replicated, as said below
Outputs:
- updated: float32 [2048, 131072], P(('col', 'row'))
Inputs may be any that keep to these rules, and one draw needn't show every extreme that they name: `coupling`: each of the two matrices is upper triangular with a diagonal between 0.5 and 2.
All inputs are finite; a program needn't handle non-finite values.
Results may differ from a plain program's by a relative error of at most 0.00016.
Values sent between devices are 32-bit elements; how exact they have to be, the bound alone decides.
No kernel may reach another device: no remote copies, remote signals or barrier semaphores. Data moves between devices by JAX's collectives and lax.ppermute only.
A program may use at most 128 MiB of HBM per device.

v0:
```python
import jax
import jax.numpy as jnp
from jax import lax
from jax.sharding import PartitionSpec as P


def full_product(former, latter, contract_dims):
    return lax.dot_general(
        former,
        latter,
        (contract_dims, ((), ())),
        precision=lax.Precision.HIGHEST,
        preferred_element_type=jnp.float32,
    )


def coupled(projection, factor):
    return full_product(projection, factor, ((1,), (1,)))


def apply_apart(eigvecs, block_list, reflect_one):
    current = eigvecs
    for vectors, factor in block_list:
        local_proj = full_product(current, vectors, ((1,), (0,)))
        reflected = reflect_one(local_proj, factor)
        current = current - full_product(reflected, vectors, ((1,), (1,)))
    return current


def body(eigvecs, basis, coupling):
    panels = lax.all_gather(basis, "col", axis=2, tiled=True)
    inner_vectors = panels[1]
    outer_vectors = panels[0]
    block_list = ((inner_vectors, coupling[1]), (outer_vectors, coupling[0]))

    def reflect_whole(local_proj, factor):
        return coupled(lax.psum(local_proj, "row"), factor)

    current = apply_apart(eigvecs, block_list, reflect_whole)
    return lax.all_to_all(current, "row", split_axis=0, concat_axis=1, tiled=True)


def solution(mesh):
    placed = (P("col", "row"), P(None, "row", "col"), P())
    return jax.shard_map(
        body, mesh=mesh, in_specs=placed, out_specs=P(("col", "row"), None), check_vma=False
    )
```

profile of v0, /device:TPU:0, one launch (start us, length us, event | category | flops | bytes accessed | tf_op | source)
XLA Modules:
  0.0 521.0 jit_solution(17176852193532060768)
XLA Ops:
  6.5 0.0 all-gather.2.cloned.1.call-start
  6.5 0.7 all-gather.2.cloned.1.call-update
  7.3 0.0 copy-start
  7.3 0.0 all-reduce.3.cloned.1.call-start
  7.3 190.7 %all-gather.2.cloned.1.call-done = f32[2,16384,256]{1,2,0:T(8,128)} async-done(((f32[2,16384,16]{1,2,0:T(8,128)}), f32[2,16384,256]{1,2,0:T(8,128)}) %all-gather.2.cloned.1.call-update) | async-done | bytes 33554448 | tf_op jit(solution)/shard_map/all_gather | solution.py:31
  198.0 20.8 %fusion = f32[128,256]{1,0:T(8,128)} fusion(f32[128,16384]{1,0:T(8,128)} %param.3, f32[2,16384,256]{1,2,0:T(8,128)} %all-gather.2.cloned.1.call-done), kind=kOutput, calls=%fused_computation.4 | convolution fusion | flops 6442450944 | bytes 25296896 | tf_op jit(solution)/shard_map/dot_general | solution.py:8
  218.9 0.0 all-reduce.3.cloned.1.call-update
  218.9 0.0 all-reduce.5.cloned.1.call-start
  218.9 71.2 %all-reduce.3.cloned.1.call-done = f32[128,256]{1,0:T(8,128)} async-done(((f32[128,256]{1,0:T(8,128)}), f32[128,256]{1,0:T(8,128)}) %all-reduce.3.cloned.1.call-update) | async-done | bytes 131088 | tf_op jit(solution)/shard_map/psum | solution.py:37
  290.1 0.0 copy-done
  290.1 1.3 fusion.4
  291.5 16.1 %convolution_subtract_fusion.1 = f32[128,16384]{1,0:T(8,128)} fusion(f32[128,16384]{1,0:T(8,128)} %param.3, f32[128,256]{1,0:T(8,128)S(1)} %fusion.4, f32[2,16384,256]{1,2,0:T(8,128)} %all-gather.2.cloned.1.call-done), kind=kOutput, calls=%fused_computation.1 | convolution fusion | flops 6444548096 | bytes 33685504 | tf_op jit(solution)/shard_map/dot_general | solution.py:8
  307.5 20.8 %fusion.1 = f32[128,256]{1,0:T(8,128)} fusion(f32[128,16384]{1,0:T(8,128)} %convolution_subtract_fusion.1, f32[2,16384,256]{1,2,0:T(8,128)} %all-gather.2.cloned.1.call-done), kind=kOutput, calls=%fused_computation.5 | convolution fusion | flops 6442450944 | bytes 25296896 | tf_op jit(solution)/shard_map/dot_general | solution.py:8
  328.4 0.0 all-reduce.5.cloned.1.call-update
  328.4 73.1 %all-reduce.5.cloned.1.call-done = f32[128,256]{1,0:T(8,128)} async-done(((f32[128,256]{1,0:T(8,128)}), f32[128,256]{1,0:T(8,128)}) %all-reduce.5.cloned.1.call-update) | async-done | bytes 131088 | tf_op jit(solution)/shard_map/psum | solution.py:37
  401.5 1.3 fusion.2
  402.8 16.1 %convolution_subtract_fusion = f32[128,16384]{1,0:T(8,128)S(1)} fusion(f32[128,16384]{1,0:T(8,128)} %convolution_subtract_fusion.1, f32[128,256]{1,0:T(8,128)S(1)} %fusion.2, f32[2,16384,256]{1,2,0:T(8,128)} %all-gather.2.cloned.1.call-done), kind=kOutput, calls=%fused_computation | convolution fusion | flops 6444548096 | bytes 33685504 | tf_op jit(solution)/shard_map/dot_general | solution.py:8
  418.9 91.6 %all_to_all.19 = f32[8,16,16384]{2,1,0:T(8,128)S(1)} all-to-all(f32[8,16,16384]{2,1,0:T(8,128)S(1)} %bitcast.25), channel_id=1, replica_groups=mesh['row'=8,'col'=16] {'row'}, dimensions={0} | all-to-all | bytes 16777216 | tf_op jit(solution)/shard_map/all_to_all | solution.py:40
  510.5 4.0 copy.5
Async XLA Ops:
  6.5 191.5 %all-gather.2.cloned.1.call-start = ((), (), s32[]{:S(2)}) async-start(), calls=%async_computation.1 | async-start | bytes 35651584 | tf_op jit(solution)/shard_map/all_gather | solution.py:31
  7.3 282.9 %copy-start = (f32[2,256,256]{2,1,0:T(8,128)S(1)}, f32[2,256,256]{2,1,0:T(8,128)}, u32[]{:S(2)}) copy-start(f32[2,256,256]{2,1,0:T(8,128)} %param.5) | copy-start | bytes 1572868
  7.3 282.9 %all-reduce.3.cloned.1.call-start = ((), (), s32[]{:S(2)}) async-start(), calls=%async_computation.2 | async-start | bytes 262144 | tf_op jit(solution)/shard_map/psum | solution.py:37
  218.9 182.6 %all-reduce.5.cloned.1.call-start = ((), (), s32[]{:S(2)}) async-start(), calls=%async_computation.3 | async-start | bytes 262144 | tf_op jit(solution)/shard_map/psum | solution.py:37
Sparse Core Ops, SparseCore 0:
  9.9 188.1 all-gather.1
  219.0 71.0 all-reduce.2
  328.5 72.9 all-reduce.4
where the time goes:
time: 521 us
  waiting for transfers between devices  336 us (64%)
  blocking collectives  91.6 us (18%)
  matrix products  76.4 us (15%)
  between operations  13.1 us (3%)
    all_gather x1, waiting for transfers between devices, body(): panels = lax.all_gather(basis, 'col', axis=2, tiled=True)  191 us
    psum x2, waiting for transfers between devices, reflect_whole(): return coupled(lax.psum(local_proj, 'row'), factor)  144 us
    all_to_all x1, blocking collectives, body(): lax.all_to_all(current, 'row', split_axis=0, concat_axis=1, tiled=True)  91.6 us
    dot_general x6, matrix products, full_product(): lax.dot_general(former, latter, (contract_dims, ((), ())), precision=lax....  76.4 us
  transfers between devices with their start and end apart: 3, of which 3 were waited for; matrix products, arithmetic and copies ran while one was open for 0% of the time, Pallas kernels for 0%

commit v1 on v0

v1 whole, which is shorter than its diff:
```python
import jax
import jax.numpy as jnp
from jax import lax
from jax.sharding import PartitionSpec as P


def full_product(former, latter, contract_dims):
    return lax.dot_general(
        former,
        latter,
        (contract_dims, ((), ())),
        precision=lax.Precision.HIGHEST,
        preferred_element_type=jnp.float32,
    )


def body(eigvecs, basis, coupling):
    panels = lax.all_gather(basis, "col", axis=2, tiled=True)
    inner_vectors = panels[1]
    outer_vectors = panels[0]
    k = inner_vectors.shape[1]
    proj_inner = full_product(eigvecs, inner_vectors, ((1,), (0,)))
    proj_outer = full_product(eigvecs, outer_vectors, ((1,), (0,)))
    gram = full_product(inner_vectors, outer_vectors, ((0,), (0,)))
    stacked = lax.psum(jnp.concatenate([proj_inner, proj_outer, gram], axis=0), "row")
    n = proj_inner.shape[0]
    proj_inner = stacked[:n]
    proj_outer = stacked[n:2 * n]
    gram = stacked[2 * n:2 * n + k]
    reflected_inner = full_product(proj_inner, coupling[1], ((1,), (1,)))
    proj_outer = proj_outer - full_product(reflected_inner, gram, ((1,), (0,)))
    reflected_outer = full_product(proj_outer, coupling[0], ((1,), (1,)))
    current = eigvecs - full_product(reflected_inner, inner_vectors, ((1,), (1,)))
    current = current - full_product(reflected_outer, outer_vectors, ((1,), (1,)))
    return lax.all_to_all(current, "row", split_axis=0, concat_axis=1, tiled=True)


def solution(mesh):
    placed = (P("col", "row"), P(None, "row", "col"), P())
    return jax.shard_map(
        body, mesh=mesh, in_specs=placed, out_specs=P(("col", "row"), None), check_vma=False
    )
```

time: 521 us -> 468 us (0.90)
  waiting for transfers between devices: 336 us -> 264 us
  matrix products: 76.4 us -> 94.3 us
    psum x2 -> x1, waiting for transfers between devices: 144 us -> 72.4 us  [body(): lax.psum(jnp.concatenate([proj_inner, proj_outer, gram], axis=0), 'row')]
    dot_general x6 -> x8, matrix products: 76.4 us -> 94.3 us  [full_product(): lax.dot_general(former, latter, (contract_dims, ((), ())), precision=lax....]
  transfers between devices with their start and end apart: 3 -> 2, of which waited for: 3 -> 2; matrix products, arithmetic and copies ran while one was open for 0% -> 0% of each run, Pallas kernels for 0% -> 0%
where the time goes in v1:
time: 468 us
  waiting for transfers between devices  264 us (56%)
  matrix products  94.3 us (20%)
  blocking collectives  91.5 us (20%)
  between operations  13.5 us (3%)
    all_gather x1, waiting for transfers between devices, body(): panels = lax.all_gather(basis, 'col', axis=2, tiled=True)  191 us
    dot_general x8, matrix products, full_product(): lax.dot_general(former, latter, (contract_dims, ((), ())), precision=lax....  94.3 us
    all_to_all x1, blocking collectives, body(): lax.all_to_all(current, 'row', split_axis=0, concat_axis=1, tiled=True)  91.5 us
    psum x1, waiting for transfers between devices, body(): lax.psum(jnp.concatenate([proj_inner, proj_outer, gram], axis=0), 'row')  72.4 us
  transfers between devices with their start and end apart: 2, of which 2 were waited for; matrix products, arithmetic and copies ran while one was open for 0% of the time, Pallas kernels for 0%

profile of v1, /device:TPU:0, one launch (start us, length us, event | category | flops | bytes accessed | tf_op | source)
XLA Modules:
  0.0 468.1 jit_solution(2041175683925098248)
XLA Ops:
  6.5 0.0 all-gather.2.cloned.1.call-start
  6.5 0.7 all-gather.2.cloned.1.call-update
  7.3 0.0 all-reduce.2.cloned.1.call-start
  7.3 190.7 %all-gather.2.cloned.1.call-done = f32[2,16384,256]{1,2,0:T(8,128)} async-done(((f32[2,16384,16]{1,2,0:T(8,128)}), f32[2,16384,256]{1,2,0:T(8,128)}) %all-gather.2.cloned.1.call-update) | async-done | bytes 33554448 | tf_op jit(solution)/shard_map/all_gather | solution.py:18
  198.0 20.2 %fusion.2 = f32[128,256]{1,0:T(8,128)S(1)} fusion(f32[128,16384]{1,0:T(8,128)} %param.3, f32[2,16384,256]{1,2,0:T(8,128)} %all-gather.2.cloned.1.call-done), kind=kOutput, calls=%fused_computation.6 | convolution fusion | flops 6442450944 | bytes 25296896 | tf_op jit(solution)/shard_map/dot_general | solution.py:8
  218.3 20.2 %fusion.1 = f32[128,256]{1,0:T(8,128)S(1)} fusion(f32[128,16384]{1,0:T(8,128)} %param.3, f32[2,16384,256]{1,2,0:T(8,128)} %all-gather.2.cloned.1.call-done), kind=kOutput, calls=%fused_computation.5 | convolution fusion | flops 6442450944 | bytes 25296896 | tf_op jit(solution)/shard_map/dot_general | solution.py:8
  238.5 0.0 copy-start
  238.5 18.6 %fusion = f32[256,256]{1,0:T(8,128)S(1)} fusion(f32[2,16384,256]{1,2,0:T(8,128)} %all-gather.2.cloned.1.call-done), kind=kOutput, calls=%fused_computation.4 | convolution fusion | flops 12884901888 | bytes 33816576 | tf_op jit(solution)/shard_map/dot_general | solution.py:8
  257.2 0.8 pad_maximum_fusion
  258.0 0.0 all-reduce.2.cloned.1.call-update
  258.0 72.4 %all-reduce.2.cloned.1.call-done = f32[512,256]{1,0:T(8,128)} async-done(((f32[512,256]{1,0:T(8,128)}), f32[512,256]{1,0:T(8,128)}) %all-reduce.2.cloned.1.call-update) | async-done | bytes 524304 | tf_op jit(solution)/shard_map/psum | solution.py:25
  330.5 0.0 copy-done
  330.5 1.3 fusion.6
  331.8 1.3 convolution_subtract_fusion.2
  333.0 0.4 fusion.4
  333.5 16.3 %convolution_subtract_fusion.1 = f32[128,16384]{1,0:T(8,128)} fusion(f32[128,16384]{1,0:T(8,128)} %param.3, f32[128,256]{1,0:T(8,128)S(1)} %fusion.6, f32[2,16384,256]{1,2,0:T(8,128)} %all-gather.2.cloned.1.call-done), kind=kOutput, calls=%fused_computation.1 | convolution fusion | flops 6444548096 | bytes 33685504 | tf_op jit(solution)/shard_map/dot_general | solution.py:8
  349.8 15.9 %convolution_subtract_fusion = f32[128,16384]{1,0:T(8,128)S(1)} fusion(f32[128,16384]{1,0:T(8,128)} %convolution_subtract_fusion.1, f32[128,256]{1,0:T(8,128)S(1)} %fusion.4, f32[2,16384,256]{1,2,0:T(8,128)} %all-gather.2.cloned.1.call-done), kind=kOutput, calls=%fused_computation | convolution fusion | flops 6444548096 | bytes 33685504 | tf_op jit(solution)/shard_map/dot_general | solution.py:8
  365.7 91.5 %all_to_all.19 = f32[8,16,16384]{2,1,0:T(8,128)S(1)} all-to-all(f32[8,16,16384]{2,1,0:T(8,128)S(1)} %bitcast.27), channel_id=1, replica_groups=mesh['row'=8,'col'=16] {'row'}, dimensions={0} | all-to-all | bytes 16777216 | tf_op jit(solution)/shard_map/all_to_all | solution.py:35
  457.3 4.0 copy.5
Async XLA Ops:
  6.5 191.5 %all-gather.2.cloned.1.call-start = ((), (), s32[]{:S(2)}) async-start(), calls=%async_computation.1 | async-start | bytes 35651584 | tf_op jit(solution)/shard_map/all_gather | solution.py:18
  7.3 323.2 %all-reduce.2.cloned.1.call-start = ((), (), s32[]{:S(2)}) async-start(), calls=%async_computation.2 | async-start | bytes 1048576 | tf_op jit(solution)/shard_map/psum | solution.py:25
  238.5 92.0 %copy-start = (f32[2,256,256]{2,1,0:T(8,128)S(1)}, f32[2,256,256]{2,1,0:T(8,128)}, u32[]{:S(2)}) copy-start(f32[2,256,256]{2,1,0:T(8,128)} %param.5) | copy-start | bytes 1572868
Sparse Core Ops, SparseCore 0:
  9.9 188.1 all-gather.1
  258.2 72.2 all-reduce.1

commit v2 on v1

v2 whole, which is shorter than its diff:
```python
import jax
import jax.numpy as jnp
from jax import lax
from jax.sharding import PartitionSpec as P


def full_product(former, latter, contract_dims, precision=lax.Precision.HIGHEST):
    return lax.dot_general(
        former,
        latter,
        (contract_dims, ((), ())),
        precision=precision,
        preferred_element_type=jnp.float32,
    )


def large_product(former, latter, contract_dims):
    return full_product(former, latter, contract_dims, lax.Precision.HIGH)


def butterfly_sum(x, axis, size):
    step = 1
    while step < size:
        pairs = [(i, i ^ step) for i in range(size)]
        x = x + lax.ppermute(x, axis, pairs)
        step *= 2
    return x


def body(eigvecs, basis, coupling):
    panels = lax.all_gather(basis, "col", axis=2, tiled=True)
    inner_vectors = panels[1]
    outer_vectors = panels[0]
    k = inner_vectors.shape[1]
    proj_inner = large_product(eigvecs, inner_vectors, ((1,), (0,)))
    proj_outer = large_product(eigvecs, outer_vectors, ((1,), (0,)))
    gram = large_product(inner_vectors, outer_vectors, ((0,), (0,)))
    rows = lax.axis_size("row")
    stacked = butterfly_sum(jnp.concatenate([proj_inner, proj_outer, gram], axis=0), "row", rows)
    n = proj_inner.shape[0]
    proj_inner = stacked[:n]
    proj_outer = stacked[n:2 * n]
    gram = stacked[2 * n:2 * n + k]
    reflected_inner = full_product(proj_inner, coupling[1], ((1,), (1,)))
    proj_outer = proj_outer - full_product(reflected_inner, gram, ((1,), (0,)))
    reflected_outer = full_product(proj_outer, coupling[0], ((1,), (1,)))
    current = eigvecs - large_product(reflected_inner, inner_vectors, ((1,), (1,)))
    current = current - large_product(reflected_outer, outer_vectors, ((1,), (1,)))
    return lax.all_to_all(current, "row", split_axis=0, concat_axis=1, tiled=True)


def solution(mesh):
    placed = (P("col", "row"), P(None, "row", "col"), P())
    return jax.shard_map(
        body, mesh=mesh, in_specs=placed, out_specs=P(("col", "row"), None), check_vma=False
    )
```

time: 468 us -> 430 us (0.919)
  waiting for transfers between devices: 264 us -> 228 us
  matrix products: 94.3 us -> 82.6 us
  starting transfers between devices: 0.04 us -> 5.27 us
    psum x1 -> x0, waiting for transfers between devices: 72.4 us -> none  [body(): lax.psum(jnp.concatenate([proj_inner, proj_outer, gram], axis=0), 'row')]
    ppermute x0 -> x3, waiting for transfers between devices: none -> 36.1 us  [butterfly_sum(): x = x + lax.ppermute(x, axis, pairs)]
    dot_general x8, matrix products: 94.3 us -> 82.6 us  [full_product(): lax.dot_general(former, latter, (contract_dims, ((), ())), precision=prec...]
    ppermute x0 -> x3, starting transfers between devices: none -> 5.27 us  [butterfly_sum(): x = x + lax.ppermute(x, axis, pairs)]
  transfers between devices with their start and end apart: 2 -> 4, of which waited for: 2 -> 4; matrix products, arithmetic and copies ran while one was open for 0% -> 0% of each run, Pallas kernels for 0% -> 0%
where the time goes in v2:
time: 430 us; the launch traced here: 429 us
  waiting for transfers between devices  228 us (53%)
  blocking collectives  96.1 us (22%)
  matrix products  82.6 us (19%)
  between operations  13.5 us (3%)
  starting transfers between devices  5.27 us (1%)
    all_gather x1, waiting for transfers between devices, body(): panels = lax.all_gather(basis, 'col', axis=2, tiled=True)  191 us
    all_to_all x1, blocking collectives, body(): lax.all_to_all(current, 'row', split_axis=0, concat_axis=1, tiled=True)  96.1 us
    dot_general x8, matrix products, full_product(): lax.dot_general(former, latter, (contract_dims, ((), ())), precision=prec...  82.6 us
    ppermute x3, waiting for transfers between devices, butterfly_sum(): x = x + lax.ppermute(x, axis, pairs)  36.1 us
  transfers between devices with their start and end apart: 4, of which 4 were waited for; matrix products, arithmetic and copies ran while one was open for 0% of the time, Pallas kernels for 0%

profile of v2, /device:TPU:0, one launch (start us, length us, event | category | flops | bytes accessed | tf_op | source)
XLA Modules:
  0.0 429.3 jit_solution(9868728124745151453)
XLA Ops:
  6.5 0.0 all-gather.2.cloned.1.call-start
  6.5 0.7 all-gather.2.cloned.1.call-update
  7.3 190.8 %all-gather.2.cloned.1.call-done = f32[2,16384,256]{1,2,0:T(8,128)} async-done(((f32[2,16384,16]{1,2,0:T(8,128)}), f32[2,16384,256]{1,2,0:T(8,128)}) %all-gather.2.cloned.1.call-update) | async-done | bytes 33554448 | tf_op jit(solution)/shard_map/all_gather | solution.py:31
  198.0 16.6 %fusion.2 = f32[128,256]{1,0:T(8,128)S(1)} fusion(f32[128,16384]{1,0:T(8,128)} %param.3, f32[2,16384,256]{1,2,0:T(8,128)} %all-gather.2.cloned.1.call-done), kind=kOutput, calls=%fused_computation.6 | convolution fusion | flops 3221225472 | bytes 25296896 | tf_op jit(solution)/shard_map/dot_general | solution.py:8
  214.6 16.7 %fusion.1 = f32[128,256]{1,0:T(8,128)S(1)} fusion(f32[128,16384]{1,0:T(8,128)} %param.3, f32[2,16384,256]{1,2,0:T(8,128)} %all-gather.2.cloned.1.call-done), kind=kOutput, calls=%fused_computation.5 | convolution fusion | flops 3221225472 | bytes 25296896 | tf_op jit(solution)/shard_map/dot_general | solution.py:8
  231.4 0.0 copy-start
  231.4 13.4 %fusion = f32[256,256]{1,0:T(8,128)S(1)} fusion(f32[2,16384,256]{1,2,0:T(8,128)} %all-gather.2.cloned.1.call-done), kind=kOutput, calls=%fused_computation.4 | convolution fusion | flops 6442450944 | bytes 33816576 | tf_op jit(solution)/shard_map/dot_general | solution.py:8
  244.8 0.7 collective-permute-start
  245.5 13.5 %collective-permute-done = f32[512,256]{1,0:T(8,128)S(1)} collective-permute-done((f32[512,256]{1,0:T(8,128)S(1)}, f32[512,256]{1,0:T(8,128)S(1)}, u32[]{:S(2)}, u32[]{:S(2)}) %collective-permute-start) | collective-permute-done | bytes 524320 | tf_op jit(solution)/shard_map/ppermute | solution.py:25
  259.0 0.1 fusion.12
  259.1 1.6 collective-permute-start.1
  260.6 11.7 %collective-permute-done.1 = f32[512,256]{1,0:T(8,128)S(1)} collective-permute-done((f32[512,256]{1,0:T(8,128)S(1)}, f32[512,256]{1,0:T(8,128)S(1)}, u32[]{:S(2)}, u32[]{:S(2)}) %collective-permute-start.1) | collective-permute-done | bytes 524320 | tf_op jit(solution)/shard_map/ppermute | solution.py:25
  272.4 0.1 add.10
  272.4 3.1 collective-permute-start.2
  275.5 10.9 %collective-permute-done.2 = f32[512,256]{1,0:T(8,128)S(1)} collective-permute-done((f32[512,256]{1,0:T(8,128)S(1)}, f32[512,256]{1,0:T(8,128)S(1)}, u32[]{:S(2)}, u32[]{:S(2)}) %collective-permute-start.2) | collective-permute-done | bytes 524320 | tf_op jit(solution)/shard_map/ppermute | solution.py:25
  286.4 0.1 add.11
  286.5 0.0 copy-done
  286.5 0.4 fusion.7
  286.9 0.3 fusion.3
  287.2 0.4 fusion.5
  287.6 17.4 %convolution_subtract_fusion.1 = f32[128,16384]{1,0:T(8,128)} fusion(f32[128,16384]{1,0:T(8,128)} %param.3, f32[128,256]{1,0:T(8,128)S(1)} %fusion.7, f32[2,16384,256]{1,2,0:T(8,128)} %all-gather.2.cloned.1.call-done), kind=kOutput, calls=%fused_computation.1 | convolution fusion | flops 3223322624 | bytes 33685504 | tf_op jit(solution)/shard_map/dot_general | solution.py:8
  305.0 17.4 %convolution_subtract_fusion = f32[128,16384]{1,0:T(8,128)} fusion(f32[128,16384]{1,0:T(8,128)} %convolution_subtract_fusion.1, f32[128,256]{1,0:T(8,128)S(1)} %fusion.5, f32[2,16384,256]{1,2,0:T(8,128)} %all-gather.2.cloned.1.call-done), kind=kOutput, calls=%fused_computation | convolution fusion | flops 3223322624 | bytes 33685504 | tf_op jit(solution)/shard_map/dot_general | solution.py:8
  322.4 96.1 %all_to_all.19 = f32[8,16,16384]{2,1,0:T(8,128)S(1)} all-to-all(f32[8,16,16384]{2,1,0:T(8,128)} %bitcast.26), channel_id=1, replica_groups=mesh['row'=8,'col'=16] {'row'}, dimensions={0} | all-to-all | bytes 16777216 | tf_op jit(solution)/shard_map/all_to_all | solution.py:49
  418.5 4.0 copy.5
  (1 shorter events, 0.0 us)
Async XLA Ops:
  6.5 191.5 %all-gather.2.cloned.1.call-start = ((), (), s32[]{:S(2)}) async-start(), calls=%async_computation.1 | async-start | bytes 35651584 | tf_op jit(solution)/shard_map/all_gather | solution.py:31
  231.4 55.1 %copy-start = (f32[2,256,256]{2,1,0:T(8,128)S(1)}, f32[2,256,256]{2,1,0:T(8,128)}, u32[]{:S(2)}) copy-start(f32[2,256,256]{2,1,0:T(8,128)} %param.5) | copy-start | bytes 1572868
  244.8 14.2 %collective-permute-start = (f32[512,256]{1,0:T(8,128)S(1)}, f32[512,256]{1,0:T(8,128)S(1)}, u32[]{:S(2)}, u32[]{:S(2)}) collective-permute-start(f32[512,256]{1,0:T(8,128)S(1)} %pad_maximum_fusion), channel_id=1, source_target_pairs={{0,16},{16,0},{32,48},{48,32},{64,80},{80,64},{96,112},{112,96},{1... | collective-permute-start | bytes 1572872 | tf_op jit(solution)/shard_map/ppermute | solution.py:25
  259.1 13.3 %collective-permute-start.1 = (f32[512,256]{1,0:T(8,128)S(1)}, f32[512,256]{1,0:T(8,128)S(1)}, u32[]{:S(2)}, u32[]{:S(2)}) collective-permute-start(f32[512,256]{1,0:T(8,128)S(1)} %fusion.12), channel_id=1, source_target_pairs={{0,32},{16,48},{32,0},{48,16},{64,96},{80,112},{96,64},{112,80},{1... | collective-permute-start | bytes 1572872 | tf_op jit(solution)/shard_map/ppermute | solution.py:25
  272.4 13.9 %collective-permute-start.2 = (f32[512,256]{1,0:T(8,128)S(1)}, f32[512,256]{1,0:T(8,128)S(1)}, u32[]{:S(2)}, u32[]{:S(2)}) collective-permute-start(f32[512,256]{1,0:T(8,128)S(1)} %add.10), channel_id=1, source_target_pairs={{0,64},{16,80},{32,96},{48,112},{64,0},{80,16},{96,32},{112,48},{1... | collective-permute-start | bytes 1572872 | tf_op jit(solution)/shard_map/ppermute | solution.py:25
Sparse Core Ops, SparseCore 0:
  9.9 188.1 all-gather.1

commit v3 on v2

--- a/solution.py
+++ b/solution.py
@@ -28,24 +28,37 @@
 
 
 def body(eigvecs, basis, coupling):
-    panels = lax.all_gather(basis, "col", axis=2, tiled=True)
-    inner_vectors = panels[1]
-    outer_vectors = panels[0]
-    k = inner_vectors.shape[1]
-    proj_inner = large_product(eigvecs, inner_vectors, ((1,), (0,)))
-    proj_outer = large_product(eigvecs, outer_vectors, ((1,), (0,)))
-    gram = large_product(inner_vectors, outer_vectors, ((0,), (0,)))
+    local_rows = basis.shape[1]
+    half = local_rows // 2
+    pieces = ((0, half), (half, local_rows))
+    panels = [
+        lax.all_gather(basis[:, lo:hi, :], "col", axis=2, tiled=True) for lo, hi in pieces
+    ]
+    n = eigvecs.shape[0]
+    k = panels[0].shape[2]
+    proj = None
+    gram = None
+    for (lo, hi), panel in zip(pieces, panels):
+        part = large_product(eigvecs[:, lo:hi], panel, ((1,), (1,)))
+        g = large_product(panel[1], panel[0], ((0,), (0,)))
+        proj = part if proj is None else proj + part
+        gram = g if gram is None else gram + g
     rows = lax.axis_size("row")
-    stacked = butterfly_sum(jnp.concatenate([proj_inner, proj_outer, gram], axis=0), "row", rows)
-    n = proj_inner.shape[0]
+    stacked = butterfly_sum(
+        jnp.concatenate([proj[:, 1, :], proj[:, 0, :], gram], axis=0), "row", rows
+    )
     proj_inner = stacked[:n]
     proj_outer = stacked[n:2 * n]
     gram = stacked[2 * n:2 * n + k]
     reflected_inner = full_product(proj_inner, coupling[1], ((1,), (1,)))
     proj_outer = proj_outer - full_product(reflected_inner, gram, ((1,), (0,)))
     reflected_outer = full_product(proj_outer, coupling[0], ((1,), (1,)))
-    current = eigvecs - large_product(reflected_inner, inner_vectors, ((1,), (1,)))
-    current = current - large_product(reflected_outer, outer_vectors, ((1,), (1,)))
+    reflected = jnp.stack([reflected_outer, reflected_inner], axis=1)
+    halves = [
+        eigvecs[:, lo:hi] - large_product(reflected, panel, ((1, 2), (0, 2)))
+        for (lo, hi), panel in zip(pieces, panels)
+    ]
+    current = jnp.concatenate(halves, axis=1)
     return lax.all_to_all(current, "row", split_axis=0, concat_axis=1, tiled=True)
 
 

time: 430 us -> 443 us (1.030)
  waiting for transfers between devices: 228 us -> 244 us
  matrix products: 82.6 us -> 70.5 us
  local copies, waits for them, and re-layouts: 3.98 us -> 10.7 us
    all_gather x1 -> x2, waiting for transfers between devices: 191 us -> 207 us  [body(): lax.all_gather(basis[:, lo:hi, :], 'col', axis=2, tiled=True)]
    dot_general x8 -> x9, matrix products: 82.6 us -> 70.5 us  [full_product(): lax.dot_general(former, latter, (contract_dims, ((), ())), precision=prec...]
  transfers between devices with their start and end apart: 4 -> 5, of which waited for: 4 -> 5; matrix products, arithmetic and copies ran while one was open for 0% -> 3% of each run, Pallas kernels for 0% -> 0%
where the time goes in v3:
time: 443 us
  waiting for transfers between devices  244 us (55%)
  blocking collectives  96 us (22%)
  matrix products  70.5 us (16%)
  between operations  13.6 us (3%)
  local copies, waits for them, and re-layouts  10.7 us (2%)
  starting transfers between devices  5.31 us (1%)
    all_gather x2, waiting for transfers between devices, body(): lax.all_gather(basis[:, lo:hi, :], 'col', axis=2, tiled=True)  207 us
    all_to_all x1, blocking collectives, body(): lax.all_to_all(current, 'row', split_axis=0, concat_axis=1, tiled=True)  96 us
    dot_general x9, matrix products, full_product(): lax.dot_general(former, latter, (contract_dims, ((), ())), precision=prec...  70.5 us
    ppermute x3, waiting for transfers between devices, butterfly_sum(): x = x + lax.ppermute(x, axis, pairs)  36.1 us
  transfers between devices with their start and end apart: 5, of which 5 were waited for; matrix products, arithmetic and copies ran while one was open for 3% of the time, Pallas kernels for 0%

profile of v3, /device:TPU:0, one launch (start us, length us, event | category | flops | bytes accessed | tf_op | source)
XLA Modules:
  0.0 442.8 jit_solution(5188162060215882200)
XLA Ops:
  6.5 0.0 all-gather.5.cloned.1.call-start
  6.5 3.0 fusion.25
  9.6 0.0 all-gather.5.cloned.1.call-update
  9.6 0.0 all-gather.3.cloned.1.call-start
  9.7 0.7 all-gather.3.cloned.1.call-update
  10.4 110.9 %all-gather.5.cloned.1.call-done = f32[2,8192,256]{1,2,0:T(8,128)} async-done(((f32[2,8192,16]{1,2,0:T(8,128)}), f32[2,8192,256]{1,2,0:T(8,128)}) %all-gather.5.cloned.1.call-update) | async-done | bytes 16777232 | tf_op jit(solution)/shard_map/all_gather | solution.py:35
  121.2 13.2 %fusion.4 = f32[128,2,256]{2,0,1:T(8,128)S(1)} fusion(f32[2,8192,256]{1,2,0:T(8,128)} %all-gather.5.cloned.1.call-done, f32[128,16384]{1,0:T(8,128)} %param.3), kind=kOutput, calls=%fused_computation.11 | convolution fusion | flops 3221225472 | bytes 21233664 | tf_op jit(solution)/shard_map/dot_general | solution.py:8
  134.4 95.8 %all-gather.3.cloned.1.call-done = f32[2,8192,256]{1,2,0:T(8,128)} async-done(((f32[2,8192,16]{1,2,0:T(8,128)}), f32[2,8192,256]{1,2,0:T(8,128)}) %all-gather.3.cloned.1.call-update) | async-done | bytes 16777232 | tf_op jit(solution)/shard_map/all_gather | solution.py:35
  230.2 0.0 slice-start
  230.2 0.0 slice-start.1
  230.2 0.0 slice-start.2
  230.2 13.3 %fusion.11 = f32[128,2,256]{2,0,1:T(8,128)S(1)} fusion(f32[128,2,256]{2,0,1:T(8,128)S(1)} %fusion.4, f32[2,8192,256]{1,2,0:T(8,128)} %all-gather.3.cloned.1.call-done, f32[128,16384]{1,0:T(8,128)} %param.3), kind=kOutput, calls=%fused_computation.18 | convolution fusion | flops 3221291008 | bytes 21495808 | tf_op jit(solution)/shard_map/dot_general | solution.py:8
  243.6 0.0 slice-start.3
  243.6 13.5 %fusion.2 = f32[256,256]{1,0:T(8,128)S(1)} fusion(f32[2,8192,256]{1,2,0:T(8,128)} %all-gather.5.cloned.1.call-done), kind=kOutput, calls=%fused_computation.5 | convolution fusion | flops 3221225472 | bytes 17039360 | tf_op jit(solution)/shard_map/dot_general | solution.py:8
  257.1 0.0 slice-done
  257.1 0.0 slice-done.1
  257.1 0.0 slice-done.2
  257.2 0.0 slice-done.3
  257.2 0.0 copy-start
  257.2 3.7 fusion.10
  260.9 0.7 collective-permute-start
  261.6 13.5 %collective-permute-done = f32[512,256]{1,0:T(8,128)S(1)} collective-permute-done((f32[512,256]{1,0:T(8,128)S(1)}, f32[512,256]{1,0:T(8,128)S(1)}, u32[]{:S(2)}, u32[]{:S(2)}) %collective-permute-start) | collective-permute-done | bytes 524320 | tf_op jit(solution)/shard_map/ppermute | solution.py:25
  275.1 0.1 fusion.24
  275.2 1.5 collective-permute-start.1
  276.7 11.8 %collective-permute-done.1 = f32[512,256]{1,0:T(8,128)S(1)} collective-permute-done((f32[512,256]{1,0:T(8,128)S(1)}, f32[512,256]{1,0:T(8,128)S(1)}, u32[]{:S(2)}, u32[]{:S(2)}) %collective-permute-start.1) | collective-permute-done | bytes 524320 | tf_op jit(solution)/shard_map/ppermute | solution.py:25
  288.5 0.1 add.18
  288.5 3.1 collective-permute-start.2
  291.6 10.9 %collective-permute-done.2 = f32[512,256]{1,0:T(8,128)S(1)} collective-permute-done((f32[512,256]{1,0:T(8,128)S(1)}, f32[512,256]{1,0:T(8,128)S(1)}, u32[]{:S(2)}, u32[]{:S(2)}) %collective-permute-start.2) | collective-permute-done | bytes 524320 | tf_op jit(solution)/shard_map/ppermute | solution.py:25
  302.5 0.1 add.19
  302.5 0.0 copy-done
  302.6 0.4 fusion.17
  303.0 0.0 slice-start.4
  303.0 0.3 fusion.14
  303.3 0.4 convolution_bitcast_fusion.2
  303.7 0.0 slice-start.5
  303.7 12.6 %fusion.1 = f32[128,8192]{1,0:T(8,128)S(1)} fusion(f32[2,8192,256]{1,2,0:T(8,128)} %all-gather.5.cloned.1.call-done, f32[128,16384]{1,0:T(8,128)} %param.3, f32[128,1,256]{2,0,1:T(8,128)S(1)} %bitcast.60, f32[128,1,256]{2,0,1:T(8,128)S(1)} %convolution_bitcast_fusion.2), kind=kOutput, calls=%fused_computation.3 | convolution fusion | flops 3222339584 | bytes 25427968 | tf_op jit(solution)/shard_map/dot_general | solution.py:8
  316.3 0.0 slice-done.4
  316.3 0.0 slice-done.5
  316.4 13.1 %fusion = f32[128,8192]{1,0:T(8,128)} fusion(f32[2,8192,256]{1,2,0:T(8,128)} %all-gather.3.cloned.1.call-done, f32[128,16384]{1,0:T(8,128)S(1)} %bitcast.57, f32[128,1,256]{2,0,1:T(8,128)S(1)} %bitcast.61, f32[128,1,256]{2,0,1:T(8,128)S(1)} %convolution_bitcast_fusion.2), kind=kOutput, calls=%fused_computation.2 | convolution fusion | flops 3222339584 | bytes 25427968 | tf_op jit(solution)/shard_map/dot_general | solution.py:8
  329.4 2.9 pad_maximum_fusion
  332.3 96.0 %all_to_all.19 = f32[8,16,16384]{2,1,0:T(8,128)} all-to-all(f32[8,16,16384]{2,1,0:T(8,128)S(1)} %bitcast.58), channel_id=1, replica_groups=mesh['row'=8,'col'=16] {'row'}, dimensions={0} | all-to-all | bytes 16777216 | tf_op jit(solution)/shard_map/all_to_all | solution.py:62
  428.4 7.6 %copy.5 = f32[8,2,8,16384]{3,2,0,1:T(8,128)} copy(f32[8,2,8,16384]{3,2,1,0:T(8,128)} %bitcast.59) | data formatting | bytes 16777216 | tf_op jit(solution)/shard_map/all_to_all | solution.py:62
  (4 shorter events, 0.1 us)
Async XLA Ops:
  6.5 114.7 %all-gather.5.cloned.1.call-start = ((), (), s32[]{:S(2)}) async-start(), calls=%async_computation.2 | async-start | bytes 17825792 | tf_op jit(solution)/shard_map/all_gather | solution.py:35
  9.6 220.6 %all-gather.3.cloned.1.call-start = ((), (), s32[]{:S(2)}) async-start(), calls=%async_computation.1 | async-start | bytes 17825792 | tf_op jit(solution)/shard_map/all_gather | solution.py:35
  230.2 26.9 %slice-start = ((s8[16777216]{0:T(1024)(128)(4,1)}), s8[4194304]{0:T(1024)(128)(4,1)S(1)}, s32[]{:S(2)}) async-start(s8[16777216]{0:T(1024)(128)(4,1)} %bitcast.54), calls=%async_computation.3 | async-start | bytes 8388608
  230.2 26.9 %slice-start.1 = ((s8[16777216]{0:T(1024)(128)(4,1)}), s8[4194304]{0:T(1024)(128)(4,1)S(1)}, s32[]{:S(2)}) async-start(s8[16777216]{0:T(1024)(128)(4,1)} %bitcast.54), calls=%async_computation.4 | async-start | bytes 8388608
  230.2 26.9 %slice-start.2 = ((s8[16777216]{0:T(1024)(128)(4,1)}), s8[4194304]{0:T(1024)(128)(4,1)S(1)}, s32[]{:S(2)}) async-start(s8[16777216]{0:T(1024)(128)(4,1)} %bitcast.54), calls=%async_computation.5 | async-start | bytes 8388608
  243.6 13.6 %slice-start.3 = ((s8[16777216]{0:T(1024)(128)(4,1)}), s8[4194304]{0:T(1024)(128)(4,1)S(1)}, s32[]{:S(2)}) async-start(s8[16777216]{0:T(1024)(128)(4,1)} %bitcast.54), calls=%async_computation.6 | async-start | bytes 8388608
  257.2 45.4 %copy-start = (f32[2,256,256]{2,1,0:T(8,128)S(1)}, f32[2,256,256]{2,1,0:T(8,128)}, u32[]{:S(2)}) copy-start(f32[2,256,256]{2,1,0:T(8,128)} %param.5) | copy-start | bytes 1572868
  260.9 14.2 %collective-permute-start = (f32[512,256]{1,0:T(8,128)S(1)}, f32[512,256]{1,0:T(8,128)S(1)}, u32[]{:S(2)}, u32[]{:S(2)}) collective-permute-start(f32[512,256]{1,0:T(8,128)S(1)} %pad_maximum_fusion.1), channel_id=1, source_target_pairs={{0,16},{16,0},{32,48},{48,32},{64,80},{80,64},{96,112},{112,96},{1... | collective-permute-start | bytes 1572872 | tf_op jit(solution)/shard_map/ppermute | solution.py:25
  275.2 13.3 %collective-permute-start.1 = (f32[512,256]{1,0:T(8,128)S(1)}, f32[512,256]{1,0:T(8,128)S(1)}, u32[]{:S(2)}, u32[]{:S(2)}) collective-permute-start(f32[512,256]{1,0:T(8,128)S(1)} %fusion.24), channel_id=1, source_target_pairs={{0,32},{16,48},{32,0},{48,16},{64,96},{80,112},{96,64},{112,80},{1... | collective-permute-start | bytes 1572872 | tf_op jit(solution)/shard_map/ppermute | solution.py:25
  288.5 13.9 %collective-permute-start.2 = (f32[512,256]{1,0:T(8,128)S(1)}, f32[512,256]{1,0:T(8,128)S(1)}, u32[]{:S(2)}, u32[]{:S(2)}) collective-permute-start(f32[512,256]{1,0:T(8,128)S(1)} %add.18), channel_id=1, source_target_pairs={{0,64},{16,80},{32,96},{48,112},{64,0},{80,16},{96,32},{112,48},{1... | collective-permute-start | bytes 1572872 | tf_op jit(solution)/shard_map/ppermute | solution.py:25
  303.0 13.4 %slice-start.4 = ((s8[8388608]{0:T(1024)(128)(4,1)}), s8[4194304]{0:T(1024)(128)(4,1)S(1)}, s32[]{:S(2)}) async-start(s8[8388608]{0:T(1024)(128)(4,1)} %bitcast.56), calls=%async_computation.7 | async-start | bytes 8388608
  303.7 12.7 %slice-start.5 = ((s8[8388608]{0:T(1024)(128)(4,1)}), s8[4194304]{0:T(1024)(128)(4,1)S(1)}, s32[]{:S(2)}) async-start(s8[8388608]{0:T(1024)(128)(4,1)} %bitcast.56), calls=%async_computation.8 | async-start | bytes 8388608
Sparse Core Ops, SparseCore 0:
  9.9 111.3 all-gather.4
  123.8 106.4 all-gather.2

commit v4 on v2

--- a/solution.py
+++ b/solution.py
@@ -28,24 +28,23 @@
 
 
 def body(eigvecs, basis, coupling):
-    panels = lax.all_gather(basis, "col", axis=2, tiled=True)
-    inner_vectors = panels[1]
-    outer_vectors = panels[0]
-    k = inner_vectors.shape[1]
-    proj_inner = large_product(eigvecs, inner_vectors, ((1,), (0,)))
-    proj_outer = large_product(eigvecs, outer_vectors, ((1,), (0,)))
-    gram = large_product(inner_vectors, outer_vectors, ((0,), (0,)))
+    panel = lax.all_gather(basis, "col", axis=2, tiled=True)
+    n = eigvecs.shape[0]
+    k = panel.shape[2]
+    proj = large_product(eigvecs, panel, ((1,), (1,)))
+    gram = large_product(panel[1], panel[0], ((0,), (0,)))
     rows = lax.axis_size("row")
-    stacked = butterfly_sum(jnp.concatenate([proj_inner, proj_outer, gram], axis=0), "row", rows)
-    n = proj_inner.shape[0]
+    stacked = butterfly_sum(
+        jnp.concatenate([proj[:, 1, :], proj[:, 0, :], gram], axis=0), "row", rows
+    )
     proj_inner = stacked[:n]
     proj_outer = stacked[n:2 * n]
     gram = stacked[2 * n:2 * n + k]
     reflected_inner = full_product(proj_inner, coupling[1], ((1,), (1,)))
     proj_outer = proj_outer - full_product(reflected_inner, gram, ((1,), (0,)))
     reflected_outer = full_product(proj_outer, coupling[0], ((1,), (1,)))
-    current = eigvecs - large_product(reflected_inner, inner_vectors, ((1,), (1,)))
-    current = current - large_product(reflected_outer, outer_vectors, ((1,), (1,)))
+    reflected = jnp.stack([reflected_outer, reflected_inner], axis=1)
+    current = eigvecs - large_product(reflected, panel, ((1, 2), (0, 2)))
     return lax.all_to_all(current, "row", split_axis=0, concat_axis=1, tiled=True)
 
 

time: 430 us -> 401 us (0.933)
  matrix products: 82.6 us -> 54.3 us
    dot_general x8 -> x6, matrix products: 82.6 us -> 54.3 us  [full_product(): lax.dot_general(former, latter, (contract_dims, ((), ())), precision=prec...]
where the time goes in v4:
time: 401 us
  waiting for transfers between devices  228 us (57%)
  blocking collectives  95.9 us (24%)
  matrix products  54.3 us (14%)
  between operations  13.5 us (3%)
  starting transfers between devices  5.45 us (1%)
    all_gather x1, waiting for transfers between devices, body(): panel = lax.all_gather(basis, 'col', axis=2, tiled=True)  191 us
    all_to_all x1, blocking collectives, body(): lax.all_to_all(current, 'row', split_axis=0, concat_axis=1, tiled=True)  95.9 us
    dot_general x6, matrix products, full_product(): lax.dot_general(former, latter, (contract_dims, ((), ())), precision=prec...  54.3 us
    ppermute x3, waiting for transfers between devices, butterfly_sum(): x = x + lax.ppermute(x, axis, pairs)  36.1 us
  transfers between devices with their start and end apart: 4, of which 4 were waited for; matrix products, arithmetic and copies ran while one was open for 0% of the time, Pallas kernels for 0%

profile of v4, /device:TPU:0, one launch (start us, length us, event | category | flops | bytes accessed | tf_op | source)
XLA Modules:
  0.0 401.0 jit_solution(17303837851828700223)
XLA Ops:
  6.5 0.0 all-gather.2.cloned.1.call-start
  6.5 0.7 all-gather.2.cloned.1.call-update
  7.3 190.8 %all-gather.2.cloned.1.call-done = f32[2,16384,256]{1,2,0:T(8,128)} async-done(((f32[2,16384,16]{1,2,0:T(8,128)}), f32[2,16384,256]{1,2,0:T(8,128)}) %all-gather.2.cloned.1.call-update) | async-done | bytes 33554448 | tf_op jit(solution)/shard_map/all_gather | solution.py:31
  198.0 22.0 %fusion.2 = f32[128,2,256]{2,0,1:T(8,128)S(1)} fusion(f32[2,16384,256]{1,2,0:T(8,128)} %all-gather.2.cloned.1.call-done, f32[128,16384]{1,0:T(8,128)} %param.3), kind=kOutput, calls=%fused_computation.5 | convolution fusion | flops 6442450944 | bytes 42205184 | tf_op jit(solution)/shard_map/dot_general | solution.py:8
  220.0 0.0 copy-start
  220.0 13.4 %fusion.1 = f32[256,256]{1,0:T(8,128)S(1)} fusion(f32[2,16384,256]{1,2,0:T(8,128)} %all-gather.2.cloned.1.call-done), kind=kOutput, calls=%fused_computation.3 | convolution fusion | flops 6442450944 | bytes 33816576 | tf_op jit(solution)/shard_map/dot_general | solution.py:8
  233.5 0.7 collective-permute-start
  234.2 13.5 %collective-permute-done = f32[512,256]{1,0:T(8,128)S(1)} collective-permute-done((f32[512,256]{1,0:T(8,128)S(1)}, f32[512,256]{1,0:T(8,128)S(1)}, u32[]{:S(2)}, u32[]{:S(2)}) %collective-permute-start) | collective-permute-done | bytes 524320 | tf_op jit(solution)/shard_map/ppermute | solution.py:25
  247.7 0.1 fusion.16
  247.8 1.5 collective-permute-start.1
  249.3 11.8 %collective-permute-done.1 = f32[512,256]{1,0:T(8,128)S(1)} collective-permute-done((f32[512,256]{1,0:T(8,128)S(1)}, f32[512,256]{1,0:T(8,128)S(1)}, u32[]{:S(2)}, u32[]{:S(2)}) %collective-permute-start.1) | collective-permute-done | bytes 524320 | tf_op jit(solution)/shard_map/ppermute | solution.py:25
  261.1 0.1 add.10
  261.1 3.2 collective-permute-start.2
  264.4 10.9 %collective-permute-done.2 = f32[512,256]{1,0:T(8,128)S(1)} collective-permute-done((f32[512,256]{1,0:T(8,128)S(1)}, f32[512,256]{1,0:T(8,128)S(1)}, u32[]{:S(2)}, u32[]{:S(2)}) %collective-permute-start.2) | collective-permute-done | bytes 524320 | tf_op jit(solution)/shard_map/ppermute | solution.py:25
  275.3 0.1 add.11
  275.3 0.0 copy-done
  275.3 0.4 fusion.10
  275.7 0.3 fusion.4
  276.0 0.4 convolution_bitcast_fusion.1
  276.4 17.8 %fusion = f32[128,16384]{1,0:T(8,128)S(1)} fusion(f32[128,16384]{1,0:T(8,128)} %param.3, f32[2,16384,256]{1,2,0:T(8,128)} %all-gather.2.cloned.1.call-done, f32[128,1,256]{2,0,1:T(8,128)S(1)} %bitcast.35, f32[128,1,256]{2,0,1:T(8,128)S(1)} %convolution_bitcast_fusion.1), kind=kOutput, calls=%fused_computation.1 | convolution fusion | flops 6444613632 | bytes 50593792 | tf_op jit(solution)/shard_map/dot_general | solution.py:8
  294.3 95.9 %all_to_all.19 = f32[8,16,16384]{2,1,0:T(8,128)S(1)} all-to-all(f32[8,16,16384]{2,1,0:T(8,128)S(1)} %bitcast.34), channel_id=1, replica_groups=mesh['row'=8,'col'=16] {'row'}, dimensions={0} | all-to-all | bytes 16777216 | tf_op jit(solution)/shard_map/all_to_all | solution.py:48
  390.2 4.0 copy.5
  (2 shorter events, 0.1 us)
Async XLA Ops:
  6.5 191.5 %all-gather.2.cloned.1.call-start = ((), (), s32[]{:S(2)}) async-start(), calls=%async_computation.1 | async-start | bytes 35651584 | tf_op jit(solution)/shard_map/all_gather | solution.py:31
  220.0 55.3 %copy-start = (f32[2,256,256]{2,1,0:T(8,128)S(1)}, f32[2,256,256]{2,1,0:T(8,128)}, u32[]{:S(2)}) copy-start(f32[2,256,256]{2,1,0:T(8,128)} %param.5) | copy-start | bytes 1572868
  233.5 14.2 %collective-permute-start = (f32[512,256]{1,0:T(8,128)S(1)}, f32[512,256]{1,0:T(8,128)S(1)}, u32[]{:S(2)}, u32[]{:S(2)}) collective-permute-start(f32[512,256]{1,0:T(8,128)S(1)} %pad_maximum_fusion), channel_id=1, source_target_pairs={{0,16},{16,0},{32,48},{48,32},{64,80},{80,64},{96,112},{112,96},{1... | collective-permute-start | bytes 1572872 | tf_op jit(solution)/shard_map/ppermute | solution.py:25
  247.8 13.3 %collective-permute-start.1 = (f32[512,256]{1,0:T(8,128)S(1)}, f32[512,256]{1,0:T(8,128)S(1)}, u32[]{:S(2)}, u32[]{:S(2)}) collective-permute-start(f32[512,256]{1,0:T(8,128)S(1)} %fusion.16), channel_id=1, source_target_pairs={{0,32},{16,48},{32,0},{48,16},{64,96},{80,112},{96,64},{112,80},{1... | collective-permute-start | bytes 1572872 | tf_op jit(solution)/shard_map/ppermute | solution.py:25
  261.1 14.1 %collective-permute-start.2 = (f32[512,256]{1,0:T(8,128)S(1)}, f32[512,256]{1,0:T(8,128)S(1)}, u32[]{:S(2)}, u32[]{:S(2)}) collective-permute-start(f32[512,256]{1,0:T(8,128)S(1)} %add.10), channel_id=1, source_target_pairs={{0,64},{16,80},{32,96},{48,112},{64,0},{80,16},{96,32},{112,48},{1... | collective-permute-start | bytes 1572872 | tf_op jit(solution)/shard_map/ppermute | solution.py:25
Sparse Core Ops, SparseCore 0:
  9.9 188.1 all-gather.1

commit v5 on v4

--- a/solution.py
+++ b/solution.py
@@ -44,8 +44,23 @@
     proj_outer = proj_outer - full_product(reflected_inner, gram, ((1,), (0,)))
     reflected_outer = full_product(proj_outer, coupling[0], ((1,), (1,)))
     reflected = jnp.stack([reflected_outer, reflected_inner], axis=1)
-    current = eigvecs - large_product(reflected, panel, ((1, 2), (0, 2)))
-    return lax.all_to_all(current, "row", split_axis=0, concat_axis=1, tiled=True)
+    me = lax.axis_index("row")
+    block_rows = n // rows
+    width = eigvecs.shape[1]
+    half = width // 2
+    updated = jnp.zeros((block_rows, rows * width), eigvecs.dtype)
+    for lo in (0, half):
+        current = eigvecs[:, lo:lo + half] - large_product(
+            reflected, panel[:, lo:lo + half, :], ((1, 2), (0, 2))
+        )
+        for shift in range(rows):
+            dest = (me + shift) % rows
+            src = (me - shift) % rows
+            block = lax.dynamic_slice_in_dim(current, dest * block_rows, block_rows, axis=0)
+            if shift:
+                block = lax.ppermute(block, "row", [(i, (i + shift) % rows) for i in range(rows)])
+            updated = lax.dynamic_update_slice_in_dim(updated, block, src * width + lo, axis=1)
+    return updated
 
 
 def solution(mesh):

time: 401 us -> 426 us (1.062)
  blocking collectives: 95.9 us -> 0 us
  starting transfers between devices: 5.45 us -> 72 us
  waiting for transfers between devices: 228 us -> 264 us
  local copies, waits for them, and re-layouts: 4 us -> 17.5 us
    all_to_all x1 -> x0, blocking collectives: 95.9 us -> none  [body(): lax.all_to_all(current, 'row', split_axis=0, concat_axis=1, tiled=True)]
    ppermute x0 -> x14, starting transfers between devices: none -> 66.5 us  [body(): lax.ppermute(block, 'row', [(i, (i + shift) % rows) for i in range(rows)])]
    ppermute x0 -> x14, waiting for transfers between devices: none -> 35.9 us  [body(): lax.ppermute(block, 'row', [(i, (i + shift) % rows) for i in range(rows)])]
    dynamic_update_slice x0 -> x14, local copies, waits for them, and re-layouts: none -> 13.7 us  [body(): lax.dynamic_update_slice_in_dim(updated, block, src * width + lo, axis=1)]
    dot_general x6 -> x7, matrix products: 54.3 us -> 57.8 us  [full_product(): lax.dot_general(former, latter, (contract_dims, ((), ())), precision=prec...]
  transfers between devices with their start and end apart: 4 -> 18, of which waited for: 4 -> 10; matrix products, arithmetic and copies ran while one was open for 0% -> 5% of each run, Pallas kernels for 0% -> 0%
where the time goes in v5:
time: 426 us; the launch traced here: 425 us
  waiting for transfers between devices  264 us (62%)
  starting transfers between devices  72 us (17%)
  matrix products  57.8 us (14%)
  local copies, waits for them, and re-layouts  17.5 us (4%)
  between operations  13.5 us (3%)
    all_gather x1, waiting for transfers between devices, body(): panel = lax.all_gather(basis, 'col', axis=2, tiled=True)  191 us
    ppermute x14, starting transfers between devices, body(): lax.ppermute(block, 'row', [(i, (i + shift) % rows) for i in range(rows)])  66.5 us
    dot_general x7, matrix products, full_product(): lax.dot_general(former, latter, (contract_dims, ((), ())), precision=prec...  57.8 us
    ppermute x3, waiting for transfers between devices, butterfly_sum(): x = x + lax.ppermute(x, axis, pairs)  36.1 us
    ppermute x14, waiting for transfers between devices, body(): lax.ppermute(block, 'row', [(i, (i + shift) % rows) for i in range(rows)])  35.9 us
    dynamic_update_slice x14, local copies, waits for them, and re-layouts, body(): lax.dynamic_update_slice_in_dim(updated, block, src * width + lo, axis=1)  13.7 us
  transfers between devices with their start and end apart: 18, of which 10 were waited for; matrix products, arithmetic and copies ran while one was open for 5% of the time, Pallas kernels for 0%

profile of v5, /device:TPU:0, one launch (start us, length us, event | category | flops | bytes accessed | tf_op | source)
XLA Modules:
  0.0 424.6 jit_solution(396658744744456172)
XLA Ops:
  6.5 0.7 all-gather.2.cloned.1.call-update
  7.3 190.8 %all-gather.2.cloned.1.call-done = f32[2,16384,256]{1,2,0:T(8,128)} async-done(((f32[2,16384,16]{1,2,0:T(8,128)}), f32[2,16384,256]{1,2,0:T(8,128)}) %all-gather.2.cloned.1.call-update) | async-done | bytes 33554448 | tf_op jit(solution)/shard_map/all_gather | solution.py:31
  198.0 22.0 %fusion.17 = f32[128,2,256]{2,0,1:T(8,128)S(1)} fusion(f32[2,16384,256]{1,2,0:T(8,128)} %all-gather.2.cloned.1.call-done, f32[128,16384]{1,0:T(8,128)} %param.3), kind=kOutput, calls=%fused_computation.11 | convolution fusion | flops 6442450944 | bytes 42205184 | tf_op jit(solution)/shard_map/dot_general | solution.py:8
  220.0 13.4 %fusion.4 = f32[256,256]{1,0:T(8,128)S(1)} fusion(f32[2,16384,256]{1,2,0:T(8,128)} %all-gather.2.cloned.1.call-done), kind=kOutput, calls=%fused_computation.5 | convolution fusion | flops 6442450944 | bytes 33816576 | tf_op jit(solution)/shard_map/dot_general | solution.py:8
  233.5 0.7 collective-permute-start
  234.2 13.5 %collective-permute-done = f32[512,256]{1,0:T(8,128)S(1)} collective-permute-done((f32[512,256]{1,0:T(8,128)S(1)}, f32[512,256]{1,0:T(8,128)S(1)}, u32[]{:S(2)}, u32[]{:S(2)}) %collective-permute-start) | collective-permute-done | bytes 524320 | tf_op jit(solution)/shard_map/ppermute | solution.py:25
  247.8 1.5 collective-permute-start.1
  249.3 11.8 %collective-permute-done.1 = f32[512,256]{1,0:T(8,128)S(1)} collective-permute-done((f32[512,256]{1,0:T(8,128)S(1)}, f32[512,256]{1,0:T(8,128)S(1)}, u32[]{:S(2)}, u32[]{:S(2)}) %collective-permute-start.1) | collective-permute-done | bytes 524320 | tf_op jit(solution)/shard_map/ppermute | solution.py:25
  261.1 3.2 collective-permute-start.2
  264.4 10.9 %collective-permute-done.2 = f32[512,256]{1,0:T(8,128)S(1)} collective-permute-done((f32[512,256]{1,0:T(8,128)S(1)}, f32[512,256]{1,0:T(8,128)S(1)}, u32[]{:S(2)}, u32[]{:S(2)}) %collective-permute-start.2) | collective-permute-done | bytes 524320 | tf_op jit(solution)/shard_map/ppermute | solution.py:25
  276.0 0.4 convolution_bitcast_fusion
  276.4 12.3 %fusion.14 = f32[128,8192]{1,0:T(8,128)S(1)} fusion(f32[2,16384,256]{1,2,0:T(8,128)} %all-gather.2.cloned.1.call-done, f32[128,16384]{1,0:T(8,128)} %param.3, f32[128,1,256]{2,0,1:T(8,128)S(1)} %bitcast.34, f32[128,1,256]{2,0,1:T(8,128)S(1)} %convolution_bitcast_fusion), kind=kOutput, calls=%fused_computation.10 | convolution fusion | flops 3222339584 | bytes 25427968 | tf_op jit(solution)/shard_map/dot_general | solution.py:8
  288.7 0.5 broadcast_in_dim.3
  289.3 1.9 constant_dynamic-slice_fusion.7
  291.2 0.6 collective-permute-start.3
  291.8 1.5 collective-permute-start.4
  293.3 3.0 collective-permute-start.5
  296.3 2.0 collective-permute-start.6
  298.3 2.1 collective-permute-start.7
  300.4 9.1 %fusion.11 = f32[128,8192]{1,0:T(8,128)S(1)} fusion(f32[2,16384,256]{1,2,0:T(8,128)} %all-gather.2.cloned.1.call-done, f32[128,16384]{1,0:T(8,128)S(1)} %bitcast.33, f32[128,1,256]{2,0,1:T(8,128)S(1)} %bitcast.35, f32[128,1,256]{2,0,1:T(8,128)S(1)} %convolution_bitcast_fusion), kind=kOutput, calls=%fused_computation.9 | convolution fusion | flops 3222339584 | bytes 25427968 | tf_op jit(solution)/shard_map/dot_general | solution.py:8
  309.5 16.9 %collective-permute-start.8 = (f32[16,8192]{1,0:T(8,128)}, f32[16,8192]{1,0:T(8,128)S(1)}, u32[]{:S(2)}, u32[]{:S(2)}) collective-permute-start(f32[16,8192]{1,0:T(8,128)} %get-tuple-element.14), channel_id=1, source_target_pairs={{0,96},{16,112},{32,0},{48,16},{64,32},{80,48},{96,64},{112,80},{1... | collective-permute-start | bytes 1572872 | tf_op jit(solution)/shard_map/ppermute | solution.py:61
  326.4 1.9 constant_dynamic-update-slice_fusion.13
  328.2 1.9 collective-permute-start.9
  330.1 1.9 constant_dynamic-update-slice_fusion.12
  332.0 10.4 %collective-permute-done.5 = f32[16,8192]{1,0:T(8,128)S(1)} collective-permute-done((f32[16,8192]{1,0:T(8,128)}, f32[16,8192]{1,0:T(8,128)S(1)}, u32[]{:S(2)}, u32[]{:S(2)}) %collective-permute-start.5) | collective-permute-done | bytes 524320 | tf_op jit(solution)/shard_map/ppermute | solution.py:61
  342.4 0.8 constant_dynamic-update-slice_fusion.11
  343.2 0.8 constant_dynamic-update-slice_fusion.10
  344.0 0.8 constant_dynamic-update-slice_fusion.9
  344.9 0.8 constant_dynamic-update-slice_fusion.8
  345.7 7.8 %collective-permute-done.9 = f32[16,8192]{1,0:T(8,128)S(1)} collective-permute-done((f32[16,8192]{1,0:T(8,128)}, f32[16,8192]{1,0:T(8,128)S(1)}, u32[]{:S(2)}, u32[]{:S(2)}) %collective-permute-start.9) | collective-permute-done | bytes 524320 | tf_op jit(solution)/shard_map/ppermute | solution.py:61
  353.5 0.8 constant_dynamic-update-slice_fusion.7
  354.3 1.3 constant_dynamic-slice_fusion
  355.6 7.2 %collective-permute-start.12 = (f32[16,8192]{1,0:T(8,128)S(1)}, f32[16,8192]{1,0:T(8,128)S(1)}, u32[]{:S(2)}, u32[]{:S(2)}) collective-permute-start(f32[16,8192]{1,0:T(8,128)S(1)} %get-tuple-element.9), channel_id=1, source_target_pairs={{0,48},{16,64},{32,80},{48,96},{64,112},{80,0},{96,16},{112,32},{1... | collective-permute-start | bytes 1572872 | tf_op jit(solution)/shard_map/ppermute | solution.py:61
  362.9 0.6 collective-permute-start.13
  363.5 4.4 %collective-permute-start.14 = (f32[16,8192]{1,0:T(8,128)S(1)}, f32[16,8192]{1,0:T(8,128)S(1)}, u32[]{:S(2)}, u32[]{:S(2)}) collective-permute-start(f32[16,8192]{1,0:T(8,128)S(1)} %get-tuple-element.7), channel_id=1, source_target_pairs={{0,80},{16,96},{32,112},{48,0},{64,16},{80,32},{96,48},{112,64},{1... | collective-permute-start | bytes 1572872 | tf_op jit(solution)/shard_map/ppermute | solution.py:61
  367.9 6.2 %collective-permute-done.10 = f32[16,8192]{1,0:T(8,128)S(1)} collective-permute-done((f32[16,8192]{1,0:T(8,128)}, f32[16,8192]{1,0:T(8,128)S(1)}, u32[]{:S(2)}, u32[]{:S(2)}) %collective-permute-start.10) | collective-permute-done | bytes 524320 | tf_op jit(solution)/shard_map/ppermute | solution.py:61
  374.1 24.5 %collective-permute-start.15 = (f32[16,8192]{1,0:T(8,128)S(1)}, f32[16,8192]{1,0:T(8,128)S(1)}, u32[]{:S(2)}, u32[]{:S(2)}) collective-permute-start(f32[16,8192]{1,0:T(8,128)S(1)} %get-tuple-element.6), channel_id=1, source_target_pairs={{0,96},{16,112},{32,0},{48,16},{64,32},{80,48},{96,64},{112,80},{1... | collective-permute-start | bytes 1572872 | tf_op jit(solution)/shard_map/ppermute | solution.py:61
  398.6 0.8 constant_dynamic-update-slice_fusion.5
  399.4 1.8 collective-permute-start.16
  401.2 0.8 constant_dynamic-update-slice_fusion.4
  402.1 6.5 %collective-permute-done.12 = f32[16,8192]{1,0:T(8,128)S(1)} collective-permute-done((f32[16,8192]{1,0:T(8,128)S(1)}, f32[16,8192]{1,0:T(8,128)S(1)}, u32[]{:S(2)}, u32[]{:S(2)}) %collective-permute-start.12) | collective-permute-done | bytes 524320 | tf_op jit(solution)/shard_map/ppermute | solution.py:61
  408.6 0.8 constant_dynamic-update-slice_fusion.3
  409.4 0.8 constant_dynamic-update-slice_fusion.2
  410.2 1.6 collective-permute-done.14
  411.9 0.8 constant_dynamic-update-slice_fusion.1
  412.7 0.8 constant_dynamic-update-slice_fusion
  413.6 3.4 collective-permute-done.16
  416.9 0.8 constant_dynamic-update-slice_fusion.6
  (27 shorter events, 1.0 us)
Async XLA Ops:
  6.5 191.5 %all-gather.2.cloned.1.call-start = ((), (), s32[]{:S(2)}) async-start(), calls=%async_computation | async-start | bytes 35651584 | tf_op jit(solution)/shard_map/all_gather | solution.py:31
  220.0 55.3 %copy-start.1 = (f32[2,256,256]{2,1,0:T(8,128)S(1)}, f32[2,256,256]{2,1,0:T(8,128)}, u32[]{:S(2)}) copy-start(f32[2,256,256]{2,1,0:T(8,128)} %param.5) | copy-start | bytes 1572868
  233.5 14.2 %collective-permute-start = (f32[512,256]{1,0:T(8,128)S(1)}, f32[512,256]{1,0:T(8,128)S(1)}, u32[]{:S(2)}, u32[]{:S(2)}) collective-permute-start(f32[512,256]{1,0:T(8,128)S(1)} %pad_maximum_fusion), channel_id=1, source_target_pairs={{0,16},{16,0},{32,48},{48,32},{64,80},{80,64},{96,112},{112,96},{1... | collective-permute-start | bytes 1572872 | tf_op jit(solution)/shard_map/ppermute | solution.py:25
  247.8 13.3 %collective-permute-start.1 = (f32[512,256]{1,0:T(8,128)S(1)}, f32[512,256]{1,0:T(8,128)S(1)}, u32[]{:S(2)}, u32[]{:S(2)}) collective-permute-start(f32[512,256]{1,0:T(8,128)S(1)} %fusion.29), channel_id=1, source_target_pairs={{0,32},{16,48},{32,0},{48,16},{64,96},{80,112},{96,64},{112,80},{1... | collective-permute-start | bytes 1572872 | tf_op jit(solution)/shard_map/ppermute | solution.py:25
  261.1 14.1 %collective-permute-start.2 = (f32[512,256]{1,0:T(8,128)S(1)}, f32[512,256]{1,0:T(8,128)S(1)}, u32[]{:S(2)}, u32[]{:S(2)}) collective-permute-start(f32[512,256]{1,0:T(8,128)S(1)} %add.228), channel_id=1, source_target_pairs={{0,64},{16,80},{32,96},{48,112},{64,0},{80,16},{96,32},{112,48},{1... | collective-permute-start | bytes 1572872 | tf_op jit(solution)/shard_map/ppermute | solution.py:25
  288.7 11.7 %slice-start = ((s8[8388608]{0:T(1024)(128)(4,1)}), s8[4194304]{0:T(1024)(128)(4,1)S(1)}, s32[]{:S(2)}) async-start(s8[8388608]{0:T(1024)(128)(4,1)} %bitcast.32), calls=%async_computation.1 | async-start | bytes 8388608
  289.3 11.1 %slice-start.1 = ((s8[8388608]{0:T(1024)(128)(4,1)}), s8[4194304]{0:T(1024)(128)(4,1)S(1)}, s32[]{:S(2)}) async-start(s8[8388608]{0:T(1024)(128)(4,1)} %bitcast.32), calls=%async_computation.2 | async-start | bytes 8388608
  291.2 7.1 %copy-start = (f32[16,131072]{1,0:T(8,128)}, f32[16,131072]{1,0:T(8,128)S(1)}, u32[]{:S(2)}) copy-start(f32[16,131072]{1,0:T(8,128)S(1)} %get-tuple-element.20) | copy-start | bytes 25165828
  291.2 18.3 %collective-permute-start.3 = (f32[16,8192]{1,0:T(8,128)}, f32[16,8192]{1,0:T(8,128)}, u32[]{:S(2)}, u32[]{:S(2)}) collective-permute-start(f32[16,8192]{1,0:T(8,128)} %get-tuple-element.19), channel_id=1, source_target_pairs={{0,16},{16,32},{32,48},{48,64},{64,80},{80,96},{96,112},{112,0},{1... | collective-permute-start | bytes 1572872 | tf_op jit(solution)/shard_map/ppermute | solution.py:61
  291.8 36.4 %collective-permute-start.4 = (f32[16,8192]{1,0:T(8,128)}, f32[16,8192]{1,0:T(8,128)}, u32[]{:S(2)}, u32[]{:S(2)}) collective-permute-start(f32[16,8192]{1,0:T(8,128)} %get-tuple-element.18), channel_id=1, source_target_pairs={{0,32},{16,48},{32,64},{48,80},{64,96},{80,112},{96,0},{112,16},{1... | collective-permute-start | bytes 1572872 | tf_op jit(solution)/shard_map/ppermute | solution.py:61
  293.3 49.0 %collective-permute-start.5 = (f32[16,8192]{1,0:T(8,128)}, f32[16,8192]{1,0:T(8,128)S(1)}, u32[]{:S(2)}, u32[]{:S(2)}) collective-permute-start(f32[16,8192]{1,0:T(8,128)} %get-tuple-element.17), channel_id=1, source_target_pairs={{0,48},{16,64},{32,80},{48,96},{64,112},{80,0},{96,16},{112,32},{1... | collective-permute-start | bytes 1572872 | tf_op jit(solution)/shard_map/ppermute | solution.py:61
  296.3 46.9 %collective-permute-start.6 = (f32[16,8192]{1,0:T(8,128)}, f32[16,8192]{1,0:T(8,128)S(1)}, u32[]{:S(2)}, u32[]{:S(2)}) collective-permute-start(f32[16,8192]{1,0:T(8,128)} %get-tuple-element.16), channel_id=1, source_target_pairs={{0,64},{16,80},{32,96},{48,112},{64,0},{80,16},{96,32},{112,48},{1... | collective-permute-start | bytes 1572872 | tf_op jit(solution)/shard_map/ppermute | solution.py:61
  298.3 45.7 %collective-permute-start.7 = (f32[16,8192]{1,0:T(8,128)}, f32[16,8192]{1,0:T(8,128)S(1)}, u32[]{:S(2)}, u32[]{:S(2)}) collective-permute-start(f32[16,8192]{1,0:T(8,128)} %get-tuple-element.15), channel_id=1, source_target_pairs={{0,80},{16,96},{32,112},{48,0},{64,16},{80,32},{96,48},{112,64},{1... | collective-permute-start | bytes 1572872 | tf_op jit(solution)/shard_map/ppermute | solution.py:61
  309.5 35.3 %collective-permute-start.8 = (f32[16,8192]{1,0:T(8,128)}, f32[16,8192]{1,0:T(8,128)S(1)}, u32[]{:S(2)}, u32[]{:S(2)}) collective-permute-start(f32[16,8192]{1,0:T(8,128)} %get-tuple-element.14), channel_id=1, source_target_pairs={{0,96},{16,112},{32,0},{48,16},{64,32},{80,48},{96,64},{112,80},{1... | collective-permute-start | bytes 1572872 | tf_op jit(solution)/shard_map/ppermute | solution.py:61
  328.2 25.3 %collective-permute-start.9 = (f32[16,8192]{1,0:T(8,128)}, f32[16,8192]{1,0:T(8,128)S(1)}, u32[]{:S(2)}, u32[]{:S(2)}) collective-permute-start(f32[16,8192]{1,0:T(8,128)} %get-tuple-element.13), channel_id=1, source_target_pairs={{0,112},{16,0},{32,16},{48,32},{64,48},{80,64},{96,80},{112,96},{1... | collective-permute-start | bytes 1572872 | tf_op jit(solution)/shard_map/ppermute | solution.py:61
  355.6 18.5 %collective-permute-start.10 = (f32[16,8192]{1,0:T(8,128)}, f32[16,8192]{1,0:T(8,128)S(1)}, u32[]{:S(2)}, u32[]{:S(2)}) collective-permute-start(f32[16,8192]{1,0:T(8,128)} %get-tuple-element.11), channel_id=1, source_target_pairs={{0,16},{16,32},{32,48},{48,64},{64,80},{80,96},{96,112},{112,0},{1... | collective-permute-start | bytes 1572872 | tf_op jit(solution)/shard_map/ppermute | solution.py:61
  355.6 43.8 %collective-permute-start.11 = (f32[16,8192]{1,0:T(8,128)}, f32[16,8192]{1,0:T(8,128)S(1)}, u32[]{:S(2)}, u32[]{:S(2)}) collective-permute-start(f32[16,8192]{1,0:T(8,128)} %get-tuple-element.10), channel_id=1, source_target_pairs={{0,32},{16,48},{32,64},{48,80},{64,96},{80,112},{96,0},{112,16},{1... | collective-permute-start | bytes 1572872 | tf_op jit(solution)/shard_map/ppermute | solution.py:61
  355.6 53.0 %collective-permute-start.12 = (f32[16,8192]{1,0:T(8,128)S(1)}, f32[16,8192]{1,0:T(8,128)S(1)}, u32[]{:S(2)}, u32[]{:S(2)}) collective-permute-start(f32[16,8192]{1,0:T(8,128)S(1)} %get-tuple-element.9), channel_id=1, source_target_pairs={{0,48},{16,64},{32,80},{48,96},{64,112},{80,0},{96,16},{112,32},{1... | collective-permute-start | bytes 1572872 | tf_op jit(solution)/shard_map/ppermute | solution.py:61
  362.9 46.6 %collective-permute-start.13 = (f32[16,8192]{1,0:T(8,128)S(1)}, f32[16,8192]{1,0:T(8,128)S(1)}, u32[]{:S(2)}, u32[]{:S(2)}) collective-permute-start(f32[16,8192]{1,0:T(8,128)S(1)} %get-tuple-element.8), channel_id=1, source_target_pairs={{0,64},{16,80},{32,96},{48,112},{64,0},{80,16},{96,32},{112,48},{1... | collective-permute-start | bytes 1572872 | tf_op jit(solution)/shard_map/ppermute | solution.py:61
  363.5 48.4 %collective-permute-start.14 = (f32[16,8192]{1,0:T(8,128)S(1)}, f32[16,8192]{1,0:T(8,128)S(1)}, u32[]{:S(2)}, u32[]{:S(2)}) collective-permute-start(f32[16,8192]{1,0:T(8,128)S(1)} %get-tuple-element.7), channel_id=1, source_target_pairs={{0,80},{16,96},{32,112},{48,0},{64,16},{80,32},{96,48},{112,64},{1... | collective-permute-start | bytes 1572872 | tf_op jit(solution)/shard_map/ppermute | solution.py:61
  374.1 38.7 %collective-permute-start.15 = (f32[16,8192]{1,0:T(8,128)S(1)}, f32[16,8192]{1,0:T(8,128)S(1)}, u32[]{:S(2)}, u32[]{:S(2)}) collective-permute-start(f32[16,8192]{1,0:T(8,128)S(1)} %get-tuple-element.6), channel_id=1, source_target_pairs={{0,96},{16,112},{32,0},{48,16},{64,32},{80,48},{96,64},{112,80},{1... | collective-permute-start | bytes 1572872 | tf_op jit(solution)/shard_map/ppermute | solution.py:61
  399.4 17.5 %collective-permute-start.16 = (f32[16,8192]{1,0:T(8,128)S(1)}, f32[16,8192]{1,0:T(8,128)S(1)}, u32[]{:S(2)}, u32[]{:S(2)}) collective-permute-start(f32[16,8192]{1,0:T(8,128)S(1)} %get-tuple-element.5), channel_id=1, source_target_pairs={{0,112},{16,0},{32,16},{48,32},{64,48},{80,64},{96,80},{112,96},{1... | collective-permute-start | bytes 1572872 | tf_op jit(solution)/shard_map/ppermute | solution.py:61
Sparse Core Ops, SparseCore 0:
  9.9 188.1 all-gather.1

commit v6 on v4

--- a/solution.py
+++ b/solution.py
@@ -1,7 +1,8 @@
 import jax
 import jax.numpy as jnp
 from jax import lax
-from jax.sharding import PartitionSpec as P
+import numpy as np
+from jax.sharding import Mesh, PartitionSpec as P
 
 
 def full_product(former, latter, contract_dims, precision=lax.Precision.HIGHEST):
@@ -28,7 +29,18 @@
 
 
 def body(eigvecs, basis, coupling):
-    panel = lax.all_gather(basis, "col", axis=2, tiled=True)
+    upper = lax.axis_index("yhi") == 1
+    partner = lax.ppermute(basis, "yhi", [(0, 1), (1, 0)])
+    lower_piece = jnp.where(upper, partner, basis)
+    upper_piece = jnp.where(upper, basis, partner)
+    panel = lax.all_gather(
+        jnp.concatenate([lower_piece, upper_piece], axis=2), "zc", axis=2, tiled=True
+    )
+    halves = lax.axis_size("yhi")
+    groups = lax.axis_size("zc")
+    piece = basis.shape[2]
+    order = np.arange(halves * groups * piece).reshape(halves, groups, piece).transpose(1, 0, 2).reshape(-1)
+    coupling = coupling[:, order][:, :, order]
     n = eigvecs.shape[0]
     k = panel.shape[2]
     proj = large_product(eigvecs, panel, ((1,), (1,)))
@@ -49,7 +61,10 @@
 
 
 def solution(mesh):
-    placed = (P("col", "row"), P(None, "row", "col"), P())
+    rows, cols = mesh.devices.shape
+    split = Mesh(mesh.devices.reshape(rows, 2, cols // 2), ("row", "yhi", "zc"))
+    col = ("yhi", "zc")
+    placed = (P(col, "row"), P(None, "row", col), P())
     return jax.shard_map(
-        body, mesh=mesh, in_specs=placed, out_specs=P(("col", "row"), None), check_vma=False
+        body, mesh=split, in_specs=placed, out_specs=P(("yhi", "zc", "row"), None), check_vma=False
     )

time: 401 us -> 422 us (1.052)
  waiting for transfers between devices: 228 us -> 236 us
  other arithmetic: 0.24 us -> 4.49 us
    ppermute x0 -> x1, waiting for transfers between devices: none -> 45.8 us  [body(): partner = lax.ppermute(basis, 'yhi', [(0, 1), (1, 0)])]
    all_gather x1, waiting for transfers between devices: 191 us -> 159 us  [body(): lax.all_gather(jnp.concatenate([lower_piece, upper_piece], axis=2), 'zc',...]
    ppermute x3, waiting for transfers between devices: 36.1 us -> 31.8 us  [butterfly_sum(): x = x + lax.ppermute(x, axis, pairs)]
  transfers between devices with their start and end apart: 4 -> 5, of which waited for: 4 -> 5; matrix products, arithmetic and copies ran while one was open for 0% -> 1% of each run, Pallas kernels for 0% -> 0%
where the time goes in v6:
time: 422 us
  waiting for transfers between devices  236 us (56%)
  blocking collectives  96.8 us (23%)
  matrix products  54.1 us (13%)
  between operations  13.5 us (3%)
  starting transfers between devices  9.66 us (2%)
  local copies, waits for them, and re-layouts  7.38 us (2%)
  other arithmetic  4.49 us (1%)
    all_gather x1, waiting for transfers between devices, body(): lax.all_gather(jnp.concatenate([lower_piece, upper_piece], axis=2), 'zc',...  159 us
    all_to_all x1, blocking collectives, body(): lax.all_to_all(current, 'row', split_axis=0, concat_axis=1, tiled=True)  96.8 us
    dot_general x6, matrix products, full_product(): lax.dot_general(former, latter, (contract_dims, ((), ())), precision=prec...  54.1 us
    ppermute x1, waiting for transfers between devices, body(): partner = lax.ppermute(basis, 'yhi', [(0, 1), (1, 0)])  45.8 us
    ppermute x3, waiting for transfers between devices, butterfly_sum(): x = x + lax.ppermute(x, axis, pairs)  31.8 us
  transfers between devices with their start and end apart: 5, of which 5 were waited for; matrix products, arithmetic and copies ran while one was open for 1% of the time, Pallas kernels for 0%

profile of v6, /device:TPU:0, one launch (start us, length us, event | category | flops | bytes accessed | tf_op | source)
XLA Modules:
  0.0 422.1 jit_solution(14610210545607243306)
XLA Ops:
  6.5 0.0 copy-start
  6.5 0.0 all-gather.2.cloned.1.call-start
  6.5 3.3 collective-permute-start
  9.8 45.8 %collective-permute-done = f32[2,16384,16]{1,2,0:T(8,128)S(1)} collective-permute-done((f32[2,16384,16]{1,2,0:T(8,128)}, f32[2,16384,16]{1,2,0:T(8,128)S(1)}, u32[]{:S(2)}, u32[]{:S(2)}) %collective-permute-start) | collective-permute-done | bytes 2097184 | tf_op jit(solution)/shard_map/ppermute | solution.py:33
  55.7 1.9 broadcast_select_fusion.1
  57.6 2.3 pad_maximum_fusion
  59.9 0.0 all-gather.2.cloned.1.call-update
  60.0 158.5 %all-gather.2.cloned.1.call-done = f32[2,16384,256]{1,2,0:T(8,128)} async-done(((f32[2,16384,32]{1,2,0:T(8,128)}), f32[2,16384,256]{1,2,0:T(8,128)}) %all-gather.2.cloned.1.call-update) | async-done | bytes 33554448 | tf_op jit(solution)/shard_map/all_gather | solution.py:36
  218.5 22.0 %fusion.4 = f32[128,2,256]{2,0,1:T(8,128)S(1)} fusion(f32[2,16384,256]{1,2,0:T(8,128)} %all-gather.2.cloned.1.call-done, f32[128,16384]{1,0:T(8,128)} %param.6), kind=kOutput, calls=%fused_computation.10 | convolution fusion | flops 6442450944 | bytes 42205184 | tf_op jit(solution)/shard_map/dot_general | solution.py:9
  240.5 0.0 copy-start.1
  240.5 13.4 %fusion.1 = f32[256,256]{1,0:T(8,128)S(1)} fusion(f32[2,16384,256]{1,2,0:T(8,128)} %all-gather.2.cloned.1.call-done), kind=kOutput, calls=%fused_computation.5 | convolution fusion | flops 6442450944 | bytes 33816576 | tf_op jit(solution)/shard_map/dot_general | solution.py:9
  254.0 1.6 collective-permute-start.1
  255.5 12.6 %collective-permute-done.1 = f32[512,256]{1,0:T(8,128)S(1)} collective-permute-done((f32[512,256]{1,0:T(8,128)S(1)}, f32[512,256]{1,0:T(8,128)S(1)}, u32[]{:S(2)}, u32[]{:S(2)}) %collective-permute-start.1) | collective-permute-done | bytes 524320 | tf_op jit(solution)/shard_map/ppermute | solution.py:26
  268.1 0.1 fusion.19
  268.2 1.5 collective-permute-start.2
  269.7 11.8 %collective-permute-done.2 = f32[512,256]{1,0:T(8,128)S(1)} collective-permute-done((f32[512,256]{1,0:T(8,128)S(1)}, f32[512,256]{1,0:T(8,128)S(1)}, u32[]{:S(2)}, u32[]{:S(2)}) %collective-permute-start.2) | collective-permute-done | bytes 524320 | tf_op jit(solution)/shard_map/ppermute | solution.py:26
  281.5 0.1 add.14
  281.6 3.2 collective-permute-start.3
  284.8 0.0 copy-done.1
  284.8 0.0 copy-done
  284.8 1.5 gather_fusion
  286.3 0.2 copy.8
  286.6 1.2 gather_fusion.1
  287.8 0.4 fusion.20
  288.2 7.5 %collective-permute-done.3 = f32[512,256]{1,0:T(8,128)S(1)} collective-permute-done((f32[512,256]{1,0:T(8,128)S(1)}, f32[512,256]{1,0:T(8,128)S(1)}, u32[]{:S(2)}, u32[]{:S(2)}) %collective-permute-start.3) | collective-permute-done | bytes 524320 | tf_op jit(solution)/shard_map/ppermute | solution.py:26
  295.7 0.1 add.15
  295.8 0.3 fusion.14
  296.1 0.3 fusion.7
  296.3 0.3 convolution_bitcast_fusion.1
  296.6 17.8 %fusion = f32[128,16384]{1,0:T(8,128)S(1)} fusion(f32[128,16384]{1,0:T(8,128)} %param.6, f32[2,16384,256]{1,2,0:T(8,128)} %all-gather.2.cloned.1.call-done, f32[128,1,256]{2,0,1:T(8,128)S(1)} %bitcast.43, f32[128,1,256]{2,0,1:T(8,128)S(1)} %convolution_bitcast_fusion.1), kind=kOutput, calls=%fused_computation.3 | convolution fusion | flops 6444613632 | bytes 50593792 | tf_op jit(solution)/shard_map/dot_general | solution.py:9
  314.5 96.8 %all_to_all.19 = f32[8,16,16384]{2,1,0:T(8,128)S(1)} all-to-all(f32[8,16,16384]{2,1,0:T(8,128)S(1)} %bitcast.40), channel_id=1, replica_groups=mesh['row'=8,'yhi'=2,'zc'=8] {'row'}, dimensions={0} | all-to-all | bytes 16777216 | tf_op jit(solution)/shard_map/all_to_all | solution.py:60
  411.3 4.0 copy.12
  (3 shorter events, 0.1 us)
Async XLA Ops:
  6.5 278.3 %copy-start = (f32[2,256,256]{2,1,0:T(8,128)S(1)}, f32[2,256,256]{2,1,0:T(8,128)}, u32[]{:S(2)}) copy-start(f32[2,256,256]{2,1,0:T(8,128)} %param.8) | copy-start | bytes 1572868
  6.5 211.9 %all-gather.2.cloned.1.call-start = ((), (), s32[]{:S(2)}) async-start(), calls=%async_computation.1 | async-start | bytes 37748736 | tf_op jit(solution)/shard_map/all_gather | solution.py:36
  6.5 49.1 %collective-permute-start = (f32[2,16384,16]{1,2,0:T(8,128)}, f32[2,16384,16]{1,2,0:T(8,128)S(1)}, u32[]{:S(2)}, u32[]{:S(2)}) collective-permute-start(f32[2,16384,16]{1,2,0:T(8,128)} %param.7), channel_id=1, source_target_pairs={{0,8},{8,0},{1,9},{9,1},{2,10},{10,2},{3,11},{11,3},{4,12},{12,4},... | collective-permute-start | bytes 6291464 | tf_op jit(solution)/shard_map/ppermute | solution.py:33
  240.5 44.3 %copy-start.1 = (s32[256]{0:T(256)S(1)}, s32[256]{0:T(256)}, u32[]{:S(2)}) copy-start(s32[256]{0:T(256)} %constant.17) | copy-start | bytes 3076
  254.0 14.2 %collective-permute-start.1 = (f32[512,256]{1,0:T(8,128)S(1)}, f32[512,256]{1,0:T(8,128)S(1)}, u32[]{:S(2)}, u32[]{:S(2)}) collective-permute-start(f32[512,256]{1,0:T(8,128)S(1)} %pad_maximum_fusion.1), channel_id=1, source_target_pairs={{0,16},{16,0},{32,48},{48,32},{64,80},{80,64},{96,112},{112,96},{1... | collective-permute-start | bytes 1572872 | tf_op jit(solution)/shard_map/ppermute | solution.py:26
  268.2 13.3 %collective-permute-start.2 = (f32[512,256]{1,0:T(8,128)S(1)}, f32[512,256]{1,0:T(8,128)S(1)}, u32[]{:S(2)}, u32[]{:S(2)}) collective-permute-start(f32[512,256]{1,0:T(8,128)S(1)} %fusion.19), channel_id=1, source_target_pairs={{0,32},{16,48},{32,0},{48,16},{64,96},{80,112},{96,64},{112,80},{1... | collective-permute-start | bytes 1572872 | tf_op jit(solution)/shard_map/ppermute | solution.py:26
  281.6 14.1 %collective-permute-start.3 = (f32[512,256]{1,0:T(8,128)S(1)}, f32[512,256]{1,0:T(8,128)S(1)}, u32[]{:S(2)}, u32[]{:S(2)}) collective-permute-start(f32[512,256]{1,0:T(8,128)S(1)} %add.14), channel_id=1, source_target_pairs={{0,64},{16,80},{32,96},{48,112},{64,0},{80,16},{96,32},{112,48},{1... | collective-permute-start | bytes 1572872 | tf_op jit(solution)/shard_map/ppermute | solution.py:26
Sparse Core Ops, SparseCore 0:
  60.1 158.3 all-gather.1

commit v7 on v4

--- a/solution.py
+++ b/solution.py
@@ -1,6 +1,8 @@
 import jax
 import jax.numpy as jnp
 from jax import lax
+from jax.experimental import pallas as pl
+from jax.experimental.pallas import tpu as pltpu
 from jax.sharding import PartitionSpec as P
 
 
@@ -27,15 +29,53 @@
     return x
 
 
+def _split(x):
+    hi = x.astype(jnp.bfloat16)
+    lo = (x - hi.astype(jnp.float32)).astype(jnp.bfloat16)
+    return hi, lo
+
+def _dot_nt(a, b):
+    return lax.dot_general(a, b, (((1,), (1,)), ((), ())), preferred_element_type=jnp.float32)
+
+def _dot3(a, b):
+    return _dot_nt(a[0], b[0]) + _dot_nt(a[0], b[1]) + _dot_nt(a[1], b[0])
+
+def _proj_kernel(e_ref, v_ref, proj_ref, gram_ref):
+    @pl.when(pl.program_id(0) == 0)
+    def _():
+        proj_ref[...] = jnp.zeros_like(proj_ref)
+        gram_ref[...] = jnp.zeros_like(gram_ref)
+    e = _split(e_ref[...])
+    outer = _split(v_ref[0])
+    inner = _split(v_ref[1])
+    proj_ref[0] += _dot3(e, outer)
+    proj_ref[1] += _dot3(e, inner)
+    gram_ref[...] += _dot3(inner, outer)
+
+def project(eigvecs, panel_t, tile):
+    n, m = eigvecs.shape
+    k = panel_t.shape[1]
+    return pl.pallas_call(
+        _proj_kernel,
+        grid=(m // tile,),
+        in_specs=[pl.BlockSpec((n, tile), lambda i: (0, i)),
+                  pl.BlockSpec((2, k, tile), lambda i: (0, 0, i))],
+        out_specs=[pl.BlockSpec((2, n, k), lambda i: (0, 0, 0)),
+                   pl.BlockSpec((k, k), lambda i: (0, 0))],
+        out_shape=[jax.ShapeDtypeStruct((2, n, k), jnp.float32),
+                   jax.ShapeDtypeStruct((k, k), jnp.float32)],
+        compiler_params=pltpu.CompilerParams(dimension_semantics=("arbitrary",)),
+    )(eigvecs, panel_t)
+
+
 def body(eigvecs, basis, coupling):
-    panel = lax.all_gather(basis, "col", axis=2, tiled=True)
+    panel = lax.all_gather(jnp.swapaxes(basis, 1, 2), "col", axis=1, tiled=True)
     n = eigvecs.shape[0]
-    k = panel.shape[2]
-    proj = large_product(eigvecs, panel, ((1,), (1,)))
-    gram = large_product(panel[1], panel[0], ((0,), (0,)))
+    k = panel.shape[1]
+    proj, gram = project(eigvecs, panel, 2048)
     rows = lax.axis_size("row")
     stacked = butterfly_sum(
-        jnp.concatenate([proj[:, 1, :], proj[:, 0, :], gram], axis=0), "row", rows
+        jnp.concatenate([proj[1], proj[0], gram], axis=0), "row", rows
     )
     proj_inner = stacked[:n]
     proj_outer = stacked[n:2 * n]
@@ -44,7 +84,7 @@
     proj_outer = proj_outer - full_product(reflected_inner, gram, ((1,), (0,)))
     reflected_outer = full_product(proj_outer, coupling[0], ((1,), (1,)))
     reflected = jnp.stack([reflected_outer, reflected_inner], axis=1)
-    current = eigvecs - large_product(reflected, panel, ((1, 2), (0, 2)))
+    current = eigvecs - large_product(reflected, panel, ((1, 2), (0, 1)))
     return lax.all_to_all(current, "row", split_axis=0, concat_axis=1, tiled=True)
 
 

time: 401 us -> 395 us (0.985)
  matrix products: 54.3 us -> 18.9 us
  Pallas kernels: 0 us -> 26.7 us
    dot_general x6 -> x4, matrix products: 54.3 us -> 18.9 us  [full_product(): lax.dot_general(former, latter, (contract_dims, ((), ())), precision=prec...]
    pallas_call x0 -> x1, Pallas kernels: none -> 26.7 us  [project(): pl.pallas_call(_proj_kernel, grid=(m // tile,), in_specs=[pl.BlockSpec((n...]
where the time goes in v7:
time: 395 us
  waiting for transfers between devices  228 us (58%)
  blocking collectives  95.9 us (24%)
  Pallas kernels  26.7 us (7%)
  matrix products  18.9 us (5%)
  between operations  13.5 us (3%)
  starting transfers between devices  5.27 us (1%)
  local copies, waits for them, and re-layouts  4.96 us (1%)
    all_gather x1, waiting for transfers between devices, body(): panel = lax.all_gather(jnp.swapaxes(basis, 1, 2), 'col', axis=1, tiled=True)  191 us
    all_to_all x1, blocking collectives, body(): lax.all_to_all(current, 'row', split_axis=0, concat_axis=1, tiled=True)  95.9 us
    ppermute x3, waiting for transfers between devices, butterfly_sum(): x = x + lax.ppermute(x, axis, pairs)  36.1 us
    pallas_call x1, Pallas kernels, project(): pl.pallas_call(_proj_kernel, grid=(m // tile,), in_specs=[pl.BlockSpec((n...  26.7 us
    dot_general x4, matrix products, full_product(): lax.dot_general(former, latter, (contract_dims, ((), ())), precision=prec...  18.9 us
  transfers between devices with their start and end apart: 4, of which 4 were waited for; matrix products, arithmetic and copies ran while one was open for 0% of the time, Pallas kernels for 0%

profile of v7, /device:TPU:0, one launch (start us, length us, event | category | flops | bytes accessed | tf_op | source)
XLA Modules:
  0.0 394.9 jit_solution(8420137712173228546)
XLA Ops:
  6.5 0.0 all-gather.2.cloned.1.call-start
  6.5 0.7 all-gather.2.cloned.1.call-update
  7.3 0.0 copy-start
  7.3 190.8 %all-gather.2.cloned.1.call-done.v_ref = f32[2,256,16384]{2,1,0:T(8,128)} async-done(((f32[2,16,16384]{2,1,0:T(8,128)}), f32[2,256,16384]{2,1,0:T(8,128)}) %all-gather.2.cloned.1.call-update) | async-done | bytes 33554448 | tf_op jit(solution)/shard_map/all_gather | solution.py:72
  198.0 26.7 %shard_map.37 = (f32[2,128,256]{2,1,0:T(8,128)}, f32[256,256]{1,0:T(8,128)}) custom-call(f32[128,16384]{1,0:T(8,128)} %e_ref.1, f32[2,256,16384]{2,1,0:T(8,128)} %all-gather.2.cloned.1.call-done.v_ref), custom_call_target="tpu_custom_call" | custom-call | tf_op jit(solution)/shard_map/pallas_call | solution.py:58
  224.7 1.0 slice_bitcast_fusion.1
  225.7 1.0 pad_maximum_fusion
  226.7 0.7 collective-permute-start
  227.3 13.5 %collective-permute-done = f32[512,256]{1,0:T(8,128)S(1)} collective-permute-done((f32[512,256]{1,0:T(8,128)S(1)}, f32[512,256]{1,0:T(8,128)S(1)}, u32[]{:S(2)}, u32[]{:S(2)}) %collective-permute-start) | collective-permute-done | bytes 524320 | tf_op jit(solution)/shard_map/ppermute | solution.py:27
  240.8 1.0 fusion.13
  241.9 1.6 collective-permute-start.1
  243.4 11.7 %collective-permute-done.1 = f32[512,256]{1,0:T(8,128)S(1)} collective-permute-done((f32[512,256]{1,0:T(8,128)S(1)}, f32[512,256]{1,0:T(8,128)S(1)}, u32[]{:S(2)}, u32[]{:S(2)}) %collective-permute-start.1) | collective-permute-done | bytes 524320 | tf_op jit(solution)/shard_map/ppermute | solution.py:27
  255.2 0.1 add.10
  255.2 3.1 collective-permute-start.2
  258.3 10.9 %collective-permute-done.2 = f32[512,256]{1,0:T(8,128)S(1)} collective-permute-done((f32[512,256]{1,0:T(8,128)S(1)}, f32[512,256]{1,0:T(8,128)S(1)}, u32[]{:S(2)}, u32[]{:S(2)}) %collective-permute-start.2) | collective-permute-done | bytes 524320 | tf_op jit(solution)/shard_map/ppermute | solution.py:27
  269.2 0.1 add.11
  269.2 0.0 copy-done
  269.3 0.4 fusion.7
  269.7 0.3 fusion.1
  270.0 0.4 convolution_bitcast_fusion.1
  270.4 17.8 %fusion = f32[128,16384]{1,0:T(8,128)S(1)} fusion(f32[128,16384]{1,0:T(8,128)} %e_ref.1, f32[2,256,16384]{2,1,0:T(8,128)} %all-gather.2.cloned.1.call-done.v_ref, f32[128,1,256]{2,0,1:T(8,128)S(1)} %bitcast.27, f32[128,1,256]{2,0,1:T(8,128)S(1)} %convolution_bitcast_fusion.1), kind=kOutput, calls=%fused_computation.1 | convolution fusion | flops 6444613632 | bytes 50593792 | tf_op jit(solution)/shard_map/dot_general | solution.py:10
  288.2 95.9 %all_to_all.19 = f32[8,16,16384]{2,1,0:T(8,128)S(1)} all-to-all(f32[8,16,16384]{2,1,0:T(8,128)S(1)} %bitcast.25), channel_id=1, replica_groups=mesh['row'=8,'col'=16] {'row'}, dimensions={0} | all-to-all | bytes 16777216 | tf_op jit(solution)/shard_map/all_to_all | solution.py:88
  384.1 4.0 %copy.5 = f32[8,2,8,16384]{3,2,0,1:T(8,128)} copy(f32[8,2,8,16384]{3,2,1,0:T(8,128)S(1)} %bitcast.24) | data formatting | bytes 16777216 | tf_op jit(solution)/shard_map/all_to_all | solution.py:88
Async XLA Ops:
  6.5 191.5 %all-gather.2.cloned.1.call-start = ((), (), s32[]{:S(2)}) async-start(), calls=%async_computation.1 | async-start | bytes 35651584 | tf_op jit(solution)/shard_map/all_gather | solution.py:72
  7.3 262.0 %copy-start = (f32[2,256,256]{2,1,0:T(8,128)S(1)}, f32[2,256,256]{2,1,0:T(8,128)}, u32[]{:S(2)}) copy-start(f32[2,256,256]{2,1,0:T(8,128)} %param.5) | copy-start | bytes 1572868
  226.7 14.2 %collective-permute-start = (f32[512,256]{1,0:T(8,128)S(1)}, f32[512,256]{1,0:T(8,128)S(1)}, u32[]{:S(2)}, u32[]{:S(2)}) collective-permute-start(f32[512,256]{1,0:T(8,128)S(1)} %pad_maximum_fusion), channel_id=1, source_target_pairs={{0,16},{16,0},{32,48},{48,32},{64,80},{80,64},{96,112},{112,96},{1... | collective-permute-start | bytes 1572872 | tf_op jit(solution)/shard_map/ppermute | solution.py:27
  241.9 13.3 %collective-permute-start.1 = (f32[512,256]{1,0:T(8,128)S(1)}, f32[512,256]{1,0:T(8,128)S(1)}, u32[]{:S(2)}, u32[]{:S(2)}) collective-permute-start(f32[512,256]{1,0:T(8,128)S(1)} %fusion.13), channel_id=1, source_target_pairs={{0,32},{16,48},{32,0},{48,16},{64,96},{80,112},{96,64},{112,80},{1... | collective-permute-start | bytes 1572872 | tf_op jit(solution)/shard_map/ppermute | solution.py:27
  255.2 13.9 %collective-permute-start.2 = (f32[512,256]{1,0:T(8,128)S(1)}, f32[512,256]{1,0:T(8,128)S(1)}, u32[]{:S(2)}, u32[]{:S(2)}) collective-permute-start(f32[512,256]{1,0:T(8,128)S(1)} %add.10), channel_id=1, source_target_pairs={{0,64},{16,80},{32,96},{48,112},{64,0},{80,16},{96,32},{112,48},{1... | collective-permute-start | bytes 1572872 | tf_op jit(solution)/shard_map/ppermute | solution.py:27
Sparse Core Ops, SparseCore 0:
  9.9 188.1 all-gather.1

commit v8 on v7

--- a/solution.py
+++ b/solution.py
@@ -40,43 +40,44 @@
 def _dot3(a, b):
     return _dot_nt(a[0], b[0]) + _dot_nt(a[0], b[1]) + _dot_nt(a[1], b[0])
 
-def _proj_kernel(e_ref, v_ref, proj_ref, gram_ref):
+def _proj_kernel(e_hi_ref, e_lo_ref, v_ref, out_ref):
     @pl.when(pl.program_id(0) == 0)
     def _():
-        proj_ref[...] = jnp.zeros_like(proj_ref)
-        gram_ref[...] = jnp.zeros_like(gram_ref)
-    e = _split(e_ref[...])
+        out_ref[...] = jnp.zeros_like(out_ref)
+    n = e_hi_ref.shape[0]
+    k = v_ref.shape[1]
+    e = (e_hi_ref[...], e_lo_ref[...])
     outer = _split(v_ref[0])
     inner = _split(v_ref[1])
-    proj_ref[0] += _dot3(e, outer)
-    proj_ref[1] += _dot3(e, inner)
-    gram_ref[...] += _dot3(inner, outer)
+    out_ref[0:n] += _dot3(e, inner)
+    out_ref[n:2 * n] += _dot3(e, outer)
+    out_ref[2 * n:2 * n + k] += _dot3(inner, outer)
+
 
 def project(eigvecs, panel_t, tile):
     n, m = eigvecs.shape
     k = panel_t.shape[1]
+    high = lax.reduce_precision(eigvecs, exponent_bits=8, mantissa_bits=7)
+    e_hi = high.astype(jnp.bfloat16)
+    e_lo = (eigvecs - high).astype(jnp.bfloat16)
     return pl.pallas_call(
         _proj_kernel,
         grid=(m // tile,),
         in_specs=[pl.BlockSpec((n, tile), lambda i: (0, i)),
+                  pl.BlockSpec((n, tile), lambda i: (0, i)),
                   pl.BlockSpec((2, k, tile), lambda i: (0, 0, i))],
-        out_specs=[pl.BlockSpec((2, n, k), lambda i: (0, 0, 0)),
-                   pl.BlockSpec((k, k), lambda i: (0, 0))],
-        out_shape=[jax.ShapeDtypeStruct((2, n, k), jnp.float32),
-                   jax.ShapeDtypeStruct((k, k), jnp.float32)],
+        out_specs=pl.BlockSpec((2 * n + k, k), lambda i: (0, 0)),
+        out_shape=jax.ShapeDtypeStruct((2 * n + k, k), jnp.float32),
         compiler_params=pltpu.CompilerParams(dimension_semantics=("arbitrary",)),
-    )(eigvecs, panel_t)
+    )(e_hi, e_lo, panel_t)
 
 
 def body(eigvecs, basis, coupling):
     panel = lax.all_gather(jnp.swapaxes(basis, 1, 2), "col", axis=1, tiled=True)
     n = eigvecs.shape[0]
     k = panel.shape[1]
-    proj, gram = project(eigvecs, panel, 2048)
     rows = lax.axis_size("row")
-    stacked = butterfly_sum(
-        jnp.concatenate([proj[1], proj[0], gram], axis=0), "row", rows
-    )
+    stacked = butterfly_sum(project(eigvecs, panel, 2048), "row", rows)
     proj_inner = stacked[:n]
     proj_outer = stacked[n:2 * n]
     gram = stacked[2 * n:2 * n + k]

time: 395 us -> 394 us (level)
  waiting for transfers between devices: 228 us -> 220 us
  other arithmetic: 2.14 us -> 9.43 us
    convert_element_type x0 -> x1, other arithmetic: none -> 8.18 us  [project(): e_lo = (eigvecs - high).astype(jnp.bfloat16)]
    all_gather x1, waiting for transfers between devices: 191 us -> 183 us  [body(): panel = lax.all_gather(jnp.swapaxes(basis, 1, 2), 'col', axis=1, tiled=True)]
  transfers between devices with their start and end apart: 4 -> 4, of which waited for: 4 -> 4; matrix products, arithmetic and copies ran while one was open for 0% -> 2% of each run, Pallas kernels for 0% -> 0%
where the time goes in v8:
time: 394 us; the launch traced here: 393 us
  waiting for transfers between devices  220 us (56%)
  blocking collectives  96 us (24%)
  Pallas kernels  26.8 us (7%)
  matrix products  18.9 us (5%)
  between operations  13.4 us (3%)
  other arithmetic  9.43 us (2%)
  starting transfers between devices  5.19 us (1%)
  local copies, waits for them, and re-layouts  3.97 us (1%)
    all_gather x1, waiting for transfers between devices, body(): panel = lax.all_gather(jnp.swapaxes(basis, 1, 2), 'col', axis=1, tiled=True)  183 us
    all_to_all x1, blocking collectives, body(): lax.all_to_all(current, 'row', split_axis=0, concat_axis=1, tiled=True)  96 us
    ppermute x3, waiting for transfers between devices, butterfly_sum(): x = x + lax.ppermute(x, axis, pairs)  36.3 us
    pallas_call x1, Pallas kernels, project(): pl.pallas_call(_proj_kernel, grid=(m // tile,), in_specs=[pl.BlockSpec((n...  26.8 us
    dot_general x4, matrix products, full_product(): lax.dot_general(former, latter, (contract_dims, ((), ())), precision=prec...  18.9 us
    convert_element_type x1, other arithmetic, project(): e_lo = (eigvecs - high).astype(jnp.bfloat16)  8.18 us
  transfers between devices with their start and end apart: 4, of which 4 were waited for; matrix products, arithmetic and copies ran while one was open for 2% of the time, Pallas kernels for 0%

profile of v8, /device:TPU:0, one launch (start us, length us, event | category | flops | bytes accessed | tf_op | source)
XLA Modules:
  0.0 393.3 jit_solution(17664946698834734466)
XLA Ops:
  6.5 0.0 all-gather.2.cloned.1.call-start
  6.5 0.7 all-gather.2.cloned.1.call-update
  7.3 8.2 %fusion.1 = (bf16[128,16384]{1,0:T(8,128)(2,1)}, bf16[128,16384]{1,0:T(8,128)(2,1)}) fusion(f32[128,16384]{1,0:T(8,128)} %param.3), kind=kLoop, calls=%fused_computation.4 | loop fusion | flops 8388608 | bytes 16777216 | tf_op jit(solution)/shard_map/convert_element_type | solution.py:62
  15.4 182.6 %all-gather.2.cloned.1.call-done.v_ref = f32[2,256,16384]{2,1,0:T(8,128)} async-done(((f32[2,16,16384]{2,1,0:T(8,128)}), f32[2,256,16384]{2,1,0:T(8,128)}) %all-gather.2.cloned.1.call-update) | async-done | bytes 33554448 | tf_op jit(solution)/shard_map/all_gather | solution.py:76
  198.0 0.0 copy-start
  198.0 26.8 %shard_map.37 = f32[512,256]{1,0:T(8,128)} custom-call(bf16[128,16384]{1,0:T(8,128)(2,1)} %get-tuple-element.6.e_hi_ref, bf16[128,16384]{1,0:T(8,128)(2,1)} %get-tuple-element.5.e_lo_ref, f32[2,256,16384]{2,1,0:T(8,128)} %all-gather.2.cloned.1.call-done.v_ref), custom_call_target="tpu_custom_call" | custom-call | tf_op jit(solution)/shard_map/pallas_call | solution.py:63
  224.8 0.6 collective-permute-start
  225.4 13.7 %collective-permute-done = f32[512,256]{1,0:T(8,128)S(1)} collective-permute-done((f32[512,256]{1,0:T(8,128)}, f32[512,256]{1,0:T(8,128)S(1)}, u32[]{:S(2)}, u32[]{:S(2)}) %collective-permute-start) | collective-permute-done | bytes 524320 | tf_op jit(solution)/shard_map/ppermute | solution.py:27
  239.1 1.1 add.9
  240.2 1.6 collective-permute-start.1
  241.8 11.7 %collective-permute-done.1 = f32[512,256]{1,0:T(8,128)S(1)} collective-permute-done((f32[512,256]{1,0:T(8,128)S(1)}, f32[512,256]{1,0:T(8,128)S(1)}, u32[]{:S(2)}, u32[]{:S(2)}) %collective-permute-start.1) | collective-permute-done | bytes 524320 | tf_op jit(solution)/shard_map/ppermute | solution.py:27
  253.5 0.1 add.10
  253.6 3.1 collective-permute-start.2
  256.6 10.9 %collective-permute-done.2 = f32[512,256]{1,0:T(8,128)S(1)} collective-permute-done((f32[512,256]{1,0:T(8,128)S(1)}, f32[512,256]{1,0:T(8,128)S(1)}, u32[]{:S(2)}, u32[]{:S(2)}) %collective-permute-start.2) | collective-permute-done | bytes 524320 | tf_op jit(solution)/shard_map/ppermute | solution.py:27
  267.5 0.1 add.11
  267.6 0.0 copy-done
  267.6 0.4 fusion.8
  268.0 0.3 fusion.2
  268.3 0.4 convolution_bitcast_fusion.1
  268.7 17.8 %fusion = f32[128,16384]{1,0:T(8,128)S(1)} fusion(f32[128,16384]{1,0:T(8,128)} %param.3, f32[2,256,16384]{2,1,0:T(8,128)} %all-gather.2.cloned.1.call-done.v_ref, f32[128,1,256]{2,0,1:T(8,128)S(1)} %bitcast.23, f32[128,1,256]{2,0,1:T(8,128)S(1)} %convolution_bitcast_fusion.1), kind=kOutput, calls=%fused_computation.1 | convolution fusion | flops 6444613632 | bytes 50593792 | tf_op jit(solution)/shard_map/dot_general | solution.py:10
  286.6 96.0 %all_to_all.19 = f32[8,16,16384]{2,1,0:T(8,128)S(1)} all-to-all(f32[8,16,16384]{2,1,0:T(8,128)S(1)} %bitcast.21), channel_id=1, replica_groups=mesh['row'=8,'col'=16] {'row'}, dimensions={0} | all-to-all | bytes 16777216 | tf_op jit(solution)/shard_map/all_to_all | solution.py:89
  382.5 4.0 %copy.5 = f32[8,2,8,16384]{3,2,0,1:T(8,128)} copy(f32[8,2,8,16384]{3,2,1,0:T(8,128)S(1)} %bitcast.20) | data formatting | bytes 16777216 | tf_op jit(solution)/shard_map/all_to_all | solution.py:89
Async XLA Ops:
  6.5 191.5 %all-gather.2.cloned.1.call-start = ((), (), s32[]{:S(2)}) async-start(), calls=%async_computation.1 | async-start | bytes 35651584 | tf_op jit(solution)/shard_map/all_gather | solution.py:76
  198.0 69.6 %copy-start = (f32[2,256,256]{2,1,0:T(8,128)S(1)}, f32[2,256,256]{2,1,0:T(8,128)}, u32[]{:S(2)}) copy-start(f32[2,256,256]{2,1,0:T(8,128)} %param.5) | copy-start | bytes 1572868
  224.8 14.3 %collective-permute-start = (f32[512,256]{1,0:T(8,128)}, f32[512,256]{1,0:T(8,128)S(1)}, u32[]{:S(2)}, u32[]{:S(2)}) collective-permute-start(f32[512,256]{1,0:T(8,128)} %shard_map.37), channel_id=1, source_target_pairs={{0,16},{16,0},{32,48},{48,32},{64,80},{80,64},{96,112},{112,96},{1... | collective-permute-start | bytes 1572872 | tf_op jit(solution)/shard_map/ppermute | solution.py:27
  240.2 13.3 %collective-permute-start.1 = (f32[512,256]{1,0:T(8,128)S(1)}, f32[512,256]{1,0:T(8,128)S(1)}, u32[]{:S(2)}, u32[]{:S(2)}) collective-permute-start(f32[512,256]{1,0:T(8,128)S(1)} %add.9), channel_id=1, source_target_pairs={{0,32},{16,48},{32,0},{48,16},{64,96},{80,112},{96,64},{112,80},{1... | collective-permute-start | bytes 1572872 | tf_op jit(solution)/shard_map/ppermute | solution.py:27
  253.6 13.9 %collective-permute-start.2 = (f32[512,256]{1,0:T(8,128)S(1)}, f32[512,256]{1,0:T(8,128)S(1)}, u32[]{:S(2)}, u32[]{:S(2)}) collective-permute-start(f32[512,256]{1,0:T(8,128)S(1)} %add.10), channel_id=1, source_target_pairs={{0,64},{16,80},{32,96},{48,112},{64,0},{80,16},{96,32},{112,48},{1... | collective-permute-start | bytes 1572872 | tf_op jit(solution)/shard_map/ppermute | solution.py:27
Sparse Core Ops, SparseCore 0:
  9.9 188.1 all-gather.1

commit v9 on v8

--- a/solution.py
+++ b/solution.py
@@ -77,7 +77,11 @@
     n = eigvecs.shape[0]
     k = panel.shape[1]
     rows = lax.axis_size("row")
-    stacked = butterfly_sum(project(eigvecs, panel, 2048), "row", rows)
+    partial = project(eigvecs, panel, 2048)
+    stacked = jnp.concatenate(
+        [butterfly_sum(partial[:2 * n], "row", rows), butterfly_sum(partial[2 * n:], "row", rows)],
+        axis=0,
+    )
     proj_inner = stacked[:n]
     proj_outer = stacked[n:2 * n]
     gram = stacked[2 * n:2 * n + k]

time: 394 us -> 393 us (level)
  waiting for transfers between devices: 220 us -> 213 us
  starting transfers between devices: 5.19 us -> 10.3 us
    ppermute x3 -> x6, waiting for transfers between devices: 36.3 us -> 30 us  [butterfly_sum(): x = x + lax.ppermute(x, axis, pairs)]
    ppermute x3 -> x6, starting transfers between devices: 5.19 us -> 10.3 us  [butterfly_sum(): x = x + lax.ppermute(x, axis, pairs)]
  transfers between devices with their start and end apart: 4 -> 7, of which waited for: 4 -> 7; matrix products, arithmetic and copies ran while one was open for 2% -> 2% of each run, Pallas kernels for 0% -> 0%
where the time goes in v9:
time: 393 us
  waiting for transfers between devices  213 us (54%)
  blocking collectives  95.6 us (24%)
  Pallas kernels  26.8 us (7%)
  matrix products  18.9 us (5%)
  between operations  13.5 us (3%)
  starting transfers between devices  10.3 us (3%)
  other arithmetic  9.38 us (2%)
  local copies, waits for them, and re-layouts  5.04 us (1%)
    all_gather x1, waiting for transfers between devices, body(): panel = lax.all_gather(jnp.swapaxes(basis, 1, 2), 'col', axis=1, tiled=True)  183 us
    all_to_all x1, blocking collectives, body(): lax.all_to_all(current, 'row', split_axis=0, concat_axis=1, tiled=True)  95.6 us
    ppermute x6, waiting for transfers between devices, butterfly_sum(): x = x + lax.ppermute(x, axis, pairs)  30 us
    pallas_call x1, Pallas kernels, project(): pl.pallas_call(_proj_kernel, grid=(m // tile,), in_specs=[pl.BlockSpec((n...  26.8 us
    dot_general x4, matrix products, full_product(): lax.dot_general(former, latter, (contract_dims, ((), ())), precision=prec...  18.9 us
    ppermute x6, starting transfers between devices, butterfly_sum(): x = x + lax.ppermute(x, axis, pairs)  10.3 us
    convert_element_type x1, other arithmetic, project(): e_lo = (eigvecs - high).astype(jnp.bfloat16)  8.18 us
  transfers between devices with their start and end apart: 7, of which 7 were waited for; matrix products, arithmetic and copies ran while one was open for 2% of the time, Pallas kernels for 0%

profile of v9, /device:TPU:0, one launch (start us, length us, event | category | flops | bytes accessed | tf_op | source)
XLA Modules:
  0.0 392.7 jit_solution(14254592275570590704)
XLA Ops:
  6.5 0.0 all-gather.2.cloned.1.call-start
  6.5 0.7 all-gather.2.cloned.1.call-update
  7.3 8.2 %fusion.1 = (bf16[128,16384]{1,0:T(8,128)(2,1)}, bf16[128,16384]{1,0:T(8,128)(2,1)}) fusion(f32[128,16384]{1,0:T(8,128)} %param.3), kind=kLoop, calls=%fused_computation.4 | loop fusion | flops 8388608 | bytes 16777216 | tf_op jit(solution)/shard_map/convert_element_type | solution.py:62
  15.4 182.6 %all-gather.2.cloned.1.call-done.v_ref = f32[2,256,16384]{2,1,0:T(8,128)} async-done(((f32[2,16,16384]{2,1,0:T(8,128)}), f32[2,256,16384]{2,1,0:T(8,128)}) %all-gather.2.cloned.1.call-update) | async-done | bytes 33554448 | tf_op jit(solution)/shard_map/all_gather | solution.py:76
  198.0 0.0 copy-start
  198.0 26.8 %shard_map.37 = f32[512,256]{1,0:T(8,128)} custom-call(bf16[128,16384]{1,0:T(8,128)(2,1)} %get-tuple-element.6.e_hi_ref, bf16[128,16384]{1,0:T(8,128)(2,1)} %get-tuple-element.5.e_lo_ref, f32[2,256,16384]{2,1,0:T(8,128)} %all-gather.2.cloned.1.call-done.v_ref), custom_call_target="tpu_custom_call" | custom-call | tf_op jit(solution)/shard_map/pallas_call | solution.py:63
  224.8 1.1 fusion.14
  225.9 0.7 collective-permute-start.3
  226.5 1.4 collective-permute-start
  228.0 7.2 %collective-permute-done.3 = f32[256,256]{1,0:T(8,128)S(1)} collective-permute-done((f32[256,256]{1,0:T(8,128)S(1)}, f32[256,256]{1,0:T(8,128)S(1)}, u32[]{:S(2)}, u32[]{:S(2)}) %collective-permute-start.3) | collective-permute-done | bytes 262176 | tf_op jit(solution)/shard_map/ppermute | solution.py:27
  235.1 4.9 %collective-permute-done = f32[256,256]{1,0:T(8,128)S(1)} collective-permute-done((f32[256,256]{1,0:T(8,128)S(1)}, f32[256,256]{1,0:T(8,128)S(1)}, u32[]{:S(2)}, u32[]{:S(2)}) %collective-permute-start) | collective-permute-done | bytes 262176 | tf_op jit(solution)/shard_map/ppermute | solution.py:27
  240.0 1.1 slice_add_fusion
  241.1 1.6 collective-permute-start.1
  242.7 0.6 collective-permute-start.4
  243.2 7.2 %collective-permute-done.1 = f32[256,256]{1,0:T(8,128)S(1)} collective-permute-done((f32[256,256]{1,0:T(8,128)S(1)}, f32[256,256]{1,0:T(8,128)S(1)}, u32[]{:S(2)}, u32[]{:S(2)}) %collective-permute-start.1) | collective-permute-done | bytes 262176 | tf_op jit(solution)/shard_map/ppermute | solution.py:27
  250.4 3.1 collective-permute-start.2
  253.5 2.5 collective-permute-done.4
  256.0 3.1 collective-permute-start.5
  259.1 4.7 %collective-permute-done.2 = f32[256,256]{1,0:T(8,128)S(1)} collective-permute-done((f32[256,256]{1,0:T(8,128)S(1)}, f32[256,256]{1,0:T(8,128)S(1)}, u32[]{:S(2)}, u32[]{:S(2)}) %collective-permute-start.2) | collective-permute-done | bytes 262176 | tf_op jit(solution)/shard_map/ppermute | solution.py:27
  263.8 0.0 copy-done
  263.8 0.4 fusion.6
  264.2 3.6 collective-permute-done.5
  267.8 0.3 fusion.9
  268.1 0.4 convolution_bitcast_fusion.1
  268.5 17.8 %fusion = f32[128,16384]{1,0:T(8,128)S(1)} fusion(f32[128,16384]{1,0:T(8,128)} %param.3, f32[2,256,16384]{2,1,0:T(8,128)} %all-gather.2.cloned.1.call-done.v_ref, f32[128,1,256]{2,0,1:T(8,128)S(1)} %bitcast.23, f32[128,1,256]{2,0,1:T(8,128)S(1)} %convolution_bitcast_fusion.1), kind=kOutput, calls=%fused_computation.1 | convolution fusion | flops 6444613632 | bytes 50593792 | tf_op jit(solution)/shard_map/dot_general | solution.py:10
  286.3 95.6 %all_to_all.19 = f32[8,16,16384]{2,1,0:T(8,128)S(1)} all-to-all(f32[8,16,16384]{2,1,0:T(8,128)S(1)} %bitcast.21), channel_id=1, replica_groups=mesh['row'=8,'col'=16] {'row'}, dimensions={0} | all-to-all | bytes 16777216 | tf_op jit(solution)/shard_map/all_to_all | solution.py:93
  381.9 4.0 %copy.5 = f32[8,2,8,16384]{3,2,0,1:T(8,128)} copy(f32[8,2,8,16384]{3,2,1,0:T(8,128)S(1)} %bitcast.20) | data formatting | bytes 16777216 | tf_op jit(solution)/shard_map/all_to_all | solution.py:93
  (3 shorter events, 0.1 us)
Async XLA Ops:
  6.5 191.5 %all-gather.2.cloned.1.call-start = ((), (), s32[]{:S(2)}) async-start(), calls=%async_computation.1 | async-start | bytes 35651584 | tf_op jit(solution)/shard_map/all_gather | solution.py:76
  198.0 65.7 %copy-start = (f32[2,256,256]{2,1,0:T(8,128)S(1)}, f32[2,256,256]{2,1,0:T(8,128)}, u32[]{:S(2)}) copy-start(f32[2,256,256]{2,1,0:T(8,128)} %param.5) | copy-start | bytes 1572868
  225.9 9.3 %collective-permute-start.3 = (f32[256,256]{1,0:T(8,128)S(1)}, f32[256,256]{1,0:T(8,128)S(1)}, u32[]{:S(2)}, u32[]{:S(2)}) collective-permute-start(f32[256,256]{1,0:T(8,128)S(1)} %get-tuple-element.9), channel_id=1, source_target_pairs={{0,16},{16,0},{32,48},{48,32},{64,80},{80,64},{96,112},{112,96},{1... | collective-permute-start | bytes 786440 | tf_op jit(solution)/shard_map/ppermute | solution.py:27
  226.5 13.5 %collective-permute-start = (f32[256,256]{1,0:T(8,128)S(1)}, f32[256,256]{1,0:T(8,128)S(1)}, u32[]{:S(2)}, u32[]{:S(2)}) collective-permute-start(f32[256,256]{1,0:T(8,128)S(1)} %get-tuple-element.10), channel_id=1, source_target_pairs={{0,16},{16,0},{32,48},{48,32},{64,80},{80,64},{96,112},{112,96},{1... | collective-permute-start | bytes 786440 | tf_op jit(solution)/shard_map/ppermute | solution.py:27
  241.1 9.3 %collective-permute-start.1 = (f32[256,256]{1,0:T(8,128)S(1)}, f32[256,256]{1,0:T(8,128)S(1)}, u32[]{:S(2)}, u32[]{:S(2)}) collective-permute-start(f32[256,256]{1,0:T(8,128)S(1)} %get-tuple-element.8), channel_id=1, source_target_pairs={{0,32},{16,48},{32,0},{48,16},{64,96},{80,112},{96,64},{112,80},{1... | collective-permute-start | bytes 786440 | tf_op jit(solution)/shard_map/ppermute | solution.py:27
  242.7 13.3 %collective-permute-start.4 = (f32[256,256]{1,0:T(8,128)S(1)}, f32[256,256]{1,0:T(8,128)S(1)}, u32[]{:S(2)}, u32[]{:S(2)}) collective-permute-start(f32[256,256]{1,0:T(8,128)S(1)} %get-tuple-element.7), channel_id=1, source_target_pairs={{0,32},{16,48},{32,0},{48,16},{64,96},{80,112},{96,64},{112,80},{1... | collective-permute-start | bytes 786440 | tf_op jit(solution)/shard_map/ppermute | solution.py:27
  250.4 13.3 %collective-permute-start.2 = (f32[256,256]{1,0:T(8,128)S(1)}, f32[256,256]{1,0:T(8,128)S(1)}, u32[]{:S(2)}, u32[]{:S(2)}) collective-permute-start(f32[256,256]{1,0:T(8,128)S(1)} %add.19), channel_id=1, source_target_pairs={{0,64},{16,80},{32,96},{48,112},{64,0},{80,16},{96,32},{112,48},{1... | collective-permute-start | bytes 786440 | tf_op jit(solution)/shard_map/ppermute | solution.py:27
  256.0 11.8 %collective-permute-start.5 = (f32[256,256]{1,0:T(8,128)S(1)}, f32[256,256]{1,0:T(8,128)S(1)}, u32[]{:S(2)}, u32[]{:S(2)}) collective-permute-start(f32[256,256]{1,0:T(8,128)S(1)} %add.22), channel_id=1, source_target_pairs={{0,64},{16,80},{32,96},{48,112},{64,0},{80,16},{96,32},{112,48},{1... | collective-permute-start | bytes 786440 | tf_op jit(solution)/shard_map/ppermute | solution.py:27
Sparse Core Ops, SparseCore 0:
  9.9 188.1 all-gather.1

commit v10 on v7

--- a/solution.py
+++ b/solution.py
@@ -24,7 +24,7 @@
     step = 1
     while step < size:
         pairs = [(i, i ^ step) for i in range(size)]
-        x = x + lax.ppermute(x, axis, pairs)
+        x = jax.tree_util.tree_map(jnp.add, x, lax.ppermute(x, axis, pairs))
         step *= 2
     return x
 
@@ -40,46 +40,51 @@
 def _dot3(a, b):
     return _dot_nt(a[0], b[0]) + _dot_nt(a[0], b[1]) + _dot_nt(a[1], b[0])
 
-def _proj_kernel(e_ref, v_ref, proj_ref, gram_ref):
+def _dot_nn(a, b):
+    return lax.dot_general(a, b, (((1,), (0,)), ((), ())), preferred_element_type=jnp.float32)
+
+
+def _proj_kernel(et_hi_ref, et_lo_ref, v_ref, pt_ref, gram_ref):
     @pl.when(pl.program_id(0) == 0)
     def _():
-        proj_ref[...] = jnp.zeros_like(proj_ref)
+        pt_ref[...] = jnp.zeros_like(pt_ref)
         gram_ref[...] = jnp.zeros_like(gram_ref)
-    e = _split(e_ref[...])
+    et = (et_hi_ref[...], et_lo_ref[...])
     outer = _split(v_ref[0])
     inner = _split(v_ref[1])
-    proj_ref[0] += _dot3(e, outer)
-    proj_ref[1] += _dot3(e, inner)
+    pt_ref[0] += _dot_nn(outer[0], et[0]) + _dot_nn(outer[0], et[1]) + _dot_nn(outer[1], et[0])
+    pt_ref[1] += _dot_nn(inner[0], et[0]) + _dot_nn(inner[0], et[1]) + _dot_nn(inner[1], et[0])
     gram_ref[...] += _dot3(inner, outer)
+
 
 def project(eigvecs, panel_t, tile):
     n, m = eigvecs.shape
     k = panel_t.shape[1]
+    high = lax.reduce_precision(eigvecs, exponent_bits=8, mantissa_bits=7)
+    et_hi = high.T.astype(jnp.bfloat16)
+    et_lo = (eigvecs - high).T.astype(jnp.bfloat16)
     return pl.pallas_call(
         _proj_kernel,
         grid=(m // tile,),
-        in_specs=[pl.BlockSpec((n, tile), lambda i: (0, i)),
+        in_specs=[pl.BlockSpec((tile, n), lambda i: (i, 0)),
+                  pl.BlockSpec((tile, n), lambda i: (i, 0)),
                   pl.BlockSpec((2, k, tile), lambda i: (0, 0, i))],
-        out_specs=[pl.BlockSpec((2, n, k), lambda i: (0, 0, 0)),
+        out_specs=[pl.BlockSpec((2, k, n), lambda i: (0, 0, 0)),
                    pl.BlockSpec((k, k), lambda i: (0, 0))],
-        out_shape=[jax.ShapeDtypeStruct((2, n, k), jnp.float32),
+        out_shape=[jax.ShapeDtypeStruct((2, k, n), jnp.float32),
                    jax.ShapeDtypeStruct((k, k), jnp.float32)],
         compiler_params=pltpu.CompilerParams(dimension_semantics=("arbitrary",)),
-    )(eigvecs, panel_t)
+    )(et_hi, et_lo, panel_t)
 
 
 def body(eigvecs, basis, coupling):
     panel = lax.all_gather(jnp.swapaxes(basis, 1, 2), "col", axis=1, tiled=True)
     n = eigvecs.shape[0]
     k = panel.shape[1]
-    proj, gram = project(eigvecs, panel, 2048)
     rows = lax.axis_size("row")
-    stacked = butterfly_sum(
-        jnp.concatenate([proj[1], proj[0], gram], axis=0), "row", rows
-    )
-    proj_inner = stacked[:n]
-    proj_outer = stacked[n:2 * n]
-    gram = stacked[2 * n:2 * n + k]
+    proj_t, gram = butterfly_sum(project(eigvecs, panel, 2048), "row", rows)
+    proj_inner = proj_t[1].T
+    proj_outer = proj_t[0].T
     reflected_inner = full_product(proj_inner, coupling[1], ((1,), (1,)))
     proj_outer = proj_outer - full_product(reflected_inner, gram, ((1,), (0,)))
     reflected_outer = full_product(proj_outer, coupling[0], ((1,), (1,)))

time: 395 us -> 384 us (0.972)
  waiting for transfers between devices: 228 us -> 199 us
  local copies, waits for them, and re-layouts: 4.96 us -> 13 us
  other arithmetic: 2.14 us -> 8.3 us
  starting transfers between devices: 5.27 us -> 11.3 us
    all_gather x1, waiting for transfers between devices: 191 us -> 176 us  [body(): panel = lax.all_gather(jnp.swapaxes(basis, 1, 2), 'col', axis=1, tiled=True)]
    ppermute x3 -> x6, waiting for transfers between devices: 36.1 us -> 22.5 us  [butterfly_sum(): x = jax.tree_util.tree_map(jnp.add, x, lax.ppermute(x, axis, pairs))]
    unnamed x2 -> x3, local copies, waits for them, and re-layouts: 0.01 us -> 8.99 us
    convert_element_type x0 -> x1, other arithmetic: none -> 6.23 us  [project(): et_lo = (eigvecs - high).T.astype(jnp.bfloat16)]
    ppermute x3 -> x6, starting transfers between devices: 5.27 us -> 11.3 us  [butterfly_sum(): x = jax.tree_util.tree_map(jnp.add, x, lax.ppermute(x, axis, pairs))]
  transfers between devices with their start and end apart: 4 -> 7, of which waited for: 4 -> 7; matrix products, arithmetic and copies ran while one was open for 0% -> 5% of each run, Pallas kernels for 0% -> 0%
where the time goes in v10:
time: 384 us
  waiting for transfers between devices  199 us (52%)
  blocking collectives  95.5 us (25%)
  Pallas kernels  24.6 us (6%)
  matrix products  19.2 us (5%)
  between operations  13.4 us (3%)
  local copies, waits for them, and re-layouts  13 us (3%)
  starting transfers between devices  11.3 us (3%)
  other arithmetic  8.3 us (2%)
    all_gather x1, waiting for transfers between devices, body(): panel = lax.all_gather(jnp.swapaxes(basis, 1, 2), 'col', axis=1, tiled=True)  176 us
    all_to_all x1, blocking collectives, body(): lax.all_to_all(current, 'row', split_axis=0, concat_axis=1, tiled=True)  95.5 us
    pallas_call x1, Pallas kernels, project(): pl.pallas_call(_proj_kernel, grid=(m // tile,), in_specs=[pl.BlockSpec((t...  24.6 us
    ppermute x6, waiting for transfers between devices, butterfly_sum(): x = jax.tree_util.tree_map(jnp.add, x, lax.ppermute(x, axis, pairs))  22.5 us
    dot_general x4, matrix products, full_product(): lax.dot_general(former, latter, (contract_dims, ((), ())), precision=prec...  19.2 us
    ppermute x6, starting transfers between devices, butterfly_sum(): x = jax.tree_util.tree_map(jnp.add, x, lax.ppermute(x, axis, pairs))  11.3 us
    unnamed x3, local copies, waits for them, and re-layouts  8.99 us
  transfers between devices with their start and end apart: 7, of which 7 were waited for; matrix products, arithmetic and copies ran while one was open for 5% of the time, Pallas kernels for 0%

profile of v10, /device:TPU:0, one launch (start us, length us, event | category | flops | bytes accessed | tf_op | source)
XLA Modules:
  0.0 384.1 jit_solution(36469258783460952)
XLA Ops:
  6.5 0.0 all-gather.2.cloned.1.call-start
  6.5 0.7 all-gather.2.cloned.1.call-update
  7.3 9.0 %copy.4 = f32[128,16384]{0,1:T(8,128)} copy(f32[128,16384]{1,0:T(8,128)} %param.3) | data formatting | bytes 16777216 | tf_op args[0]
  16.2 6.2 %fusion.2 = (bf16[16384,128]{1,0:T(8,128)(2,1)}, bf16[16384,128]{1,0:T(8,128)(2,1)}) fusion(f32[128,16384]{0,1:T(8,128)} %copy.4), kind=kLoop, calls=%fused_computation.5 | loop fusion | flops 8388608 | bytes 16777216 | tf_op jit(solution)/shard_map/convert_element_type | solution.py:65
  22.5 175.6 %all-gather.2.cloned.1.call-done.v_ref = f32[2,256,16384]{2,1,0:T(8,128)} async-done(((f32[2,16,16384]{2,1,0:T(8,128)}), f32[2,256,16384]{2,1,0:T(8,128)}) %all-gather.2.cloned.1.call-update) | async-done | bytes 33554448 | tf_op jit(solution)/shard_map/all_gather | solution.py:81
  198.0 0.0 copy-start
  198.0 24.6 %shard_map.37 = (f32[2,256,128]{2,1,0:T(8,128)}, f32[256,256]{1,0:T(8,128)}) custom-call(bf16[16384,128]{1,0:T(8,128)(2,1)} %get-tuple-element.10.et_hi_ref, bf16[16384,128]{1,0:T(8,128)(2,1)} %get-tuple-element.9.et_lo_ref, f32[2,256,16384]{2,1,0:T(8,128)} %all-gather.2.cloned.1.call-done.v_ref), custom_call_target="tpu_custom_call" | custom-call | tf_op jit(solution)/shard_map/pallas_call | solution.py:66
  222.6 0.6 collective-permute-start
  223.2 1.4 collective-permute-start.3
  224.7 7.4 %collective-permute-done = f32[2,256,128]{2,1,0:T(8,128)S(1)} collective-permute-done((f32[2,256,128]{2,1,0:T(8,128)}, f32[2,256,128]{2,1,0:T(8,128)S(1)}, u32[]{:S(2)}, u32[]{:S(2)}) %collective-permute-start) | collective-permute-done | bytes 262176 | tf_op jit(solution)/shard_map/ppermute | solution.py:27
  232.0 1.0 add.18
  233.0 1.6 collective-permute-start.1
  234.6 2.3 collective-permute-done.3
  236.9 1.0 add.21
  237.9 1.6 collective-permute-start.4
  239.5 0.5 collective-permute-done.1
  240.0 3.1 collective-permute-start.2
  243.1 4.1 %collective-permute-done.4 = f32[256,256]{1,0:T(8,128)S(1)} collective-permute-done((f32[256,256]{1,0:T(8,128)S(1)}, f32[256,256]{1,0:T(8,128)S(1)}, u32[]{:S(2)}, u32[]{:S(2)}) %collective-permute-start.4) | collective-permute-done | bytes 262176 | tf_op jit(solution)/shard_map/ppermute | solution.py:27
  247.2 3.1 collective-permute-start.5
  250.3 4.6 %collective-permute-done.2 = f32[2,256,128]{2,1,0:T(8,128)S(1)} collective-permute-done((f32[2,256,128]{2,1,0:T(8,128)S(1)}, f32[2,256,128]{2,1,0:T(8,128)S(1)}, u32[]{:S(2)}, u32[]{:S(2)}) %collective-permute-start.2) | collective-permute-done | bytes 262176 | tf_op jit(solution)/shard_map/ppermute | solution.py:27
  254.9 0.0 copy-done
  255.0 0.4 fusion.8
  255.4 3.6 collective-permute-done.5
  258.9 0.6 fusion.11
  259.5 0.4 convolution_bitcast_fusion.1
  259.9 17.8 %fusion = f32[128,16384]{1,0:T(8,128)S(1)} fusion(f32[128,16384]{1,0:T(8,128)} %param.3, f32[2,256,16384]{2,1,0:T(8,128)} %all-gather.2.cloned.1.call-done.v_ref, f32[128,1,256]{2,0,1:T(8,128)S(1)} %bitcast.37, f32[128,1,256]{2,0,1:T(8,128)S(1)} %convolution_bitcast_fusion.1), kind=kOutput, calls=%fused_computation.1 | convolution fusion | flops 6444613632 | bytes 50593792 | tf_op jit(solution)/shard_map/dot_general | solution.py:10
  277.8 95.5 %all_to_all.19 = f32[8,16,16384]{2,1,0:T(8,128)S(1)} all-to-all(f32[8,16,16384]{2,1,0:T(8,128)S(1)} %bitcast.35), channel_id=1, replica_groups=mesh['row'=8,'col'=16] {'row'}, dimensions={0} | all-to-all | bytes 16777216 | tf_op jit(solution)/shard_map/all_to_all | solution.py:93
  373.3 4.0 %copy.7 = f32[8,2,8,16384]{3,2,0,1:T(8,128)} copy(f32[8,2,8,16384]{3,2,1,0:T(8,128)S(1)} %bitcast.34) | data formatting | bytes 16777216 | tf_op jit(solution)/shard_map/all_to_all | solution.py:93
  (3 shorter events, 0.1 us)
Async XLA Ops:
  6.5 191.5 %all-gather.2.cloned.1.call-start = ((), (), s32[]{:S(2)}) async-start(), calls=%async_computation.1 | async-start | bytes 35651584 | tf_op jit(solution)/shard_map/all_gather | solution.py:81
  198.0 56.9 %copy-start = (f32[2,256,256]{2,1,0:T(8,128)S(1)}, f32[2,256,256]{2,1,0:T(8,128)}, u32[]{:S(2)}) copy-start(f32[2,256,256]{2,1,0:T(8,128)} %param.5) | copy-start | bytes 1572868
  222.6 9.4 %collective-permute-start = (f32[2,256,128]{2,1,0:T(8,128)}, f32[2,256,128]{2,1,0:T(8,128)S(1)}, u32[]{:S(2)}, u32[]{:S(2)}) collective-permute-start(f32[2,256,128]{2,1,0:T(8,128)} %get-tuple-element.7), channel_id=1, source_target_pairs={{0,16},{16,0},{32,48},{48,32},{64,80},{80,64},{96,112},{112,96},{1... | collective-permute-start | bytes 786440 | tf_op jit(solution)/shard_map/ppermute | solution.py:27
  223.2 13.7 %collective-permute-start.3 = (f32[256,256]{1,0:T(8,128)}, f32[256,256]{1,0:T(8,128)S(1)}, u32[]{:S(2)}, u32[]{:S(2)}) collective-permute-start(f32[256,256]{1,0:T(8,128)} %get-tuple-element.8), channel_id=1, source_target_pairs={{0,16},{16,0},{32,48},{48,32},{64,80},{80,64},{96,112},{112,96},{1... | collective-permute-start | bytes 786440 | tf_op jit(solution)/shard_map/ppermute | solution.py:27
  233.0 7.0 %collective-permute-start.1 = (f32[2,256,128]{2,1,0:T(8,128)S(1)}, f32[2,256,128]{2,1,0:T(8,128)S(1)}, u32[]{:S(2)}, u32[]{:S(2)}) collective-permute-start(f32[2,256,128]{2,1,0:T(8,128)S(1)} %add.18), channel_id=1, source_target_pairs={{0,32},{16,48},{32,0},{48,16},{64,96},{80,112},{96,64},{112,80},{1... | collective-permute-start | bytes 786440 | tf_op jit(solution)/shard_map/ppermute | solution.py:27
  237.9 9.3 %collective-permute-start.4 = (f32[256,256]{1,0:T(8,128)S(1)}, f32[256,256]{1,0:T(8,128)S(1)}, u32[]{:S(2)}, u32[]{:S(2)}) collective-permute-start(f32[256,256]{1,0:T(8,128)S(1)} %add.21), channel_id=1, source_target_pairs={{0,32},{16,48},{32,0},{48,16},{64,96},{80,112},{96,64},{112,80},{1... | collective-permute-start | bytes 786440 | tf_op jit(solution)/shard_map/ppermute | solution.py:27
  240.0 14.9 %collective-permute-start.2 = (f32[2,256,128]{2,1,0:T(8,128)S(1)}, f32[2,256,128]{2,1,0:T(8,128)S(1)}, u32[]{:S(2)}, u32[]{:S(2)}) collective-permute-start(f32[2,256,128]{2,1,0:T(8,128)S(1)} %add.19), channel_id=1, source_target_pairs={{0,64},{16,80},{32,96},{48,112},{64,0},{80,16},{96,32},{112,48},{1... | collective-permute-start | bytes 786440 | tf_op jit(solution)/shard_map/ppermute | solution.py:27
  247.2 11.7 %collective-permute-start.5 = (f32[256,256]{1,0:T(8,128)S(1)}, f32[256,256]{1,0:T(8,128)S(1)}, u32[]{:S(2)}, u32[]{:S(2)}) collective-permute-start(f32[256,256]{1,0:T(8,128)S(1)} %add.22), channel_id=1, source_target_pairs={{0,64},{16,80},{32,96},{48,112},{64,0},{80,16},{96,32},{112,48},{1... | collective-permute-start | bytes 786440 | tf_op jit(solution)/shard_map/ppermute | solution.py:27
Sparse Core Ops, SparseCore 0:
  9.9 188.1 all-gather.1

commit v11 on v10

--- a/solution.py
+++ b/solution.py
@@ -44,17 +44,21 @@
     return lax.dot_general(a, b, (((1,), (0,)), ((), ())), preferred_element_type=jnp.float32)
 
 
-def _proj_kernel(et_hi_ref, et_lo_ref, v_ref, pt_ref, gram_ref):
+def _proj_kernel(et_hi_ref, et_lo_ref, v_ref, outer_ref, inner_ref, gram_lo_ref, gram_hi_ref):
+    outs = (outer_ref, inner_ref, gram_lo_ref, gram_hi_ref)
+
     @pl.when(pl.program_id(0) == 0)
     def _():
-        pt_ref[...] = jnp.zeros_like(pt_ref)
-        gram_ref[...] = jnp.zeros_like(gram_ref)
+        for ref in outs:
+            ref[...] = jnp.zeros_like(ref)
     et = (et_hi_ref[...], et_lo_ref[...])
     outer = _split(v_ref[0])
     inner = _split(v_ref[1])
-    pt_ref[0] += _dot_nn(outer[0], et[0]) + _dot_nn(outer[0], et[1]) + _dot_nn(outer[1], et[0])
-    pt_ref[1] += _dot_nn(inner[0], et[0]) + _dot_nn(inner[0], et[1]) + _dot_nn(inner[1], et[0])
-    gram_ref[...] += _dot3(inner, outer)
+    outer_ref[...] += _dot_nn(outer[0], et[0]) + _dot_nn(outer[0], et[1]) + _dot_nn(outer[1], et[0])
+    inner_ref[...] += _dot_nn(inner[0], et[0]) + _dot_nn(inner[0], et[1]) + _dot_nn(inner[1], et[0])
+    half = gram_lo_ref.shape[0]
+    gram_lo_ref[...] += _dot3((inner[0][:half], inner[1][:half]), outer)
+    gram_hi_ref[...] += _dot3((inner[0][half:], inner[1][half:]), outer)
 
 
 def project(eigvecs, panel_t, tile):
@@ -69,10 +73,10 @@
         in_specs=[pl.BlockSpec((tile, n), lambda i: (i, 0)),
                   pl.BlockSpec((tile, n), lambda i: (i, 0)),
                   pl.BlockSpec((2, k, tile), lambda i: (0, 0, i))],
-        out_specs=[pl.BlockSpec((2, k, n), lambda i: (0, 0, 0)),
-                   pl.BlockSpec((k, k), lambda i: (0, 0))],
-        out_shape=[jax.ShapeDtypeStruct((2, k, n), jnp.float32),
-                   jax.ShapeDtypeStruct((k, k), jnp.float32)],
+        out_specs=[pl.BlockSpec((k, n), lambda i: (0, 0))] * 2
+        + [pl.BlockSpec((k // 2, k), lambda i: (0, 0))] * 2,
+        out_shape=[jax.ShapeDtypeStruct((k, n), jnp.float32)] * 2
+        + [jax.ShapeDtypeStruct((k // 2, k), jnp.float32)] * 2,
         compiler_params=pltpu.CompilerParams(dimension_semantics=("arbitrary",)),
     )(et_hi, et_lo, panel_t)
 
@@ -82,9 +86,10 @@
     n = eigvecs.shape[0]
     k = panel.shape[1]
     rows = lax.axis_size("row")
-    proj_t, gram = butterfly_sum(project(eigvecs, panel, 2048), "row", rows)
-    proj_inner = proj_t[1].T
-    proj_outer = proj_t[0].T
+    outer_t, inner_t, gram_lo, gram_hi = butterfly_sum(project(eigvecs, panel, 2048), "row", rows)
+    gram = jnp.concatenate([gram_lo, gram_hi], axis=0)
+    proj_inner = inner_t.T
+    proj_outer = outer_t.T
     reflected_inner = full_product(proj_inner, coupling[1], ((1,), (1,)))
     proj_outer = proj_outer - full_product(reflected_inner, gram, ((1,), (0,)))
     reflected_outer = full_product(proj_outer, coupling[0], ((1,), (1,)))

time: 384 us -> 391 us (1.018)
  waiting for transfers between devices: 199 us -> 188 us
  Pallas kernels: 24.6 us -> 33.3 us
  starting transfers between devices: 11.3 us -> 18.1 us
    ppermute x6 -> x12, waiting for transfers between devices: 22.5 us -> 11.4 us  [butterfly_sum(): x = jax.tree_util.tree_map(jnp.add, x, lax.ppermute(x, axis, pairs))]
    pallas_call x1, Pallas kernels: 24.6 us -> 33.3 us  [project(): pl.pallas_call(_proj_kernel, grid=(m // tile,), in_specs=[pl.BlockSpec((t...]
    ppermute x6 -> x12, starting transfers between devices: 11.3 us -> 18.1 us  [butterfly_sum(): x = jax.tree_util.tree_map(jnp.add, x, lax.ppermute(x, axis, pairs))]
  transfers between devices with their start and end apart: 7 -> 13, of which waited for: 7 -> 8; matrix products, arithmetic and copies ran while one was open for 5% -> 5% of each run, Pallas kernels for 0% -> 0%
where the time goes in v11:
time: 391 us
  waiting for transfers between devices  188 us (48%)
  blocking collectives  96.2 us (25%)
  Pallas kernels  33.3 us (9%)
  matrix products  19.2 us (5%)
  starting transfers between devices  18.1 us (5%)
  between operations  13.5 us (3%)
  local copies, waits for them, and re-layouts  13 us (3%)
  other arithmetic  10 us (3%)
    all_gather x1, waiting for transfers between devices, body(): panel = lax.all_gather(jnp.swapaxes(basis, 1, 2), 'col', axis=1, tiled=True)  176 us
    all_to_all x1, blocking collectives, body(): lax.all_to_all(current, 'row', split_axis=0, concat_axis=1, tiled=True)  96.2 us
    pallas_call x1, Pallas kernels, project(): pl.pallas_call(_proj_kernel, grid=(m // tile,), in_specs=[pl.BlockSpec((t...  33.3 us
    dot_general x4, matrix products, full_product(): lax.dot_general(former, latter, (contract_dims, ((), ())), precision=prec...  19.2 us
    ppermute x12, starting transfers between devices, butterfly_sum(): x = jax.tree_util.tree_map(jnp.add, x, lax.ppermute(x, axis, pairs))  18.1 us
    ppermute x12, waiting for transfers between devices, butterfly_sum(): x = jax.tree_util.tree_map(jnp.add, x, lax.ppermute(x, axis, pairs))  11.4 us
    unnamed x3, local copies, waits for them, and re-layouts  8.99 us
  transfers between devices with their start and end apart: 13, of which 8 were waited for; matrix products, arithmetic and copies ran while one was open for 5% of the time, Pallas kernels for 0%

profile of v11, /device:TPU:0, one launch (start us, length us, event | category | flops | bytes accessed | tf_op | source)
XLA Modules:
  0.0 391.0 jit_solution(6813461433091523519)
XLA Ops:
  6.5 0.0 all-gather.2.cloned.1.call-start
  6.5 0.7 all-gather.2.cloned.1.call-update
  7.3 9.0 %copy.4 = f32[128,16384]{0,1:T(8,128)} copy(f32[128,16384]{1,0:T(8,128)} %param.3) | data formatting | bytes 16777216 | tf_op args[0]
  16.2 6.2 %fusion.2 = (bf16[16384,128]{1,0:T(8,128)(2,1)}, bf16[16384,128]{1,0:T(8,128)(2,1)}) fusion(f32[128,16384]{0,1:T(8,128)} %copy.4), kind=kLoop, calls=%fused_computation.5 | loop fusion | flops 8388608 | bytes 16777216 | tf_op jit(solution)/shard_map/convert_element_type | solution.py:69
  22.5 175.6 %all-gather.2.cloned.1.call-done.v_ref = f32[2,256,16384]{2,1,0:T(8,128)} async-done(((f32[2,16,16384]{2,1,0:T(8,128)}), f32[2,256,16384]{2,1,0:T(8,128)}) %all-gather.2.cloned.1.call-update) | async-done | bytes 33554448 | tf_op jit(solution)/shard_map/all_gather | solution.py:85
  198.0 0.0 copy-start
  198.0 33.3 %shard_map.37 = (f32[256,128]{1,0:T(8,128)}, f32[256,128]{1,0:T(8,128)}, f32[128,256]{1,0:T(8,128)}, f32[128,256]{1,0:T(8,128)}) custom-call(bf16[16384,128]{1,0:T(8,128)(2,1)} %get-tuple-element.14.et_hi_ref, bf16[16384,128]{1,0:T(8,128)(2,1)} %get-tuple-element.13.et_lo_ref, f32[2,256,16384]{2,1,0:T(8,128)} %all-gather.2.cloned.1.call-done.v_ref), custom_call_target="tpu_custom_call" | custom-call | tf_op jit(solution)/shard_map/pallas_call | solution.py:70
  231.4 0.6 collective-permute-start.6
  231.9 1.4 collective-permute-start.9
  233.4 0.6 collective-permute-start.3
  234.0 1.4 collective-permute-start
  235.4 2.5 collective-permute-done.6
  237.9 0.9 add.42
  238.9 1.6 collective-permute-start.7
  240.4 0.3 collective-permute-done.9
  240.7 0.9 add.45
  241.7 1.6 collective-permute-start.10
  243.2 0.3 collective-permute-done.3
  243.6 0.9 add.39
  244.5 1.6 collective-permute-start.4
  246.0 0.0 collective-permute-done
  246.0 0.9 add.36
  247.0 1.2 collective-permute-start.1
  248.1 0.0 collective-permute-done.7
  248.1 2.8 collective-permute-start.8
  250.9 0.0 collective-permute-done.10
  250.9 0.9 collective-permute-start.11
  251.9 0.0 collective-permute-done.4
  251.9 2.8 collective-permute-start.5
  254.6 0.0 collective-permute-done.1
  254.7 1.8 collective-permute-start.2
  256.4 1.7 collective-permute-done.8
  258.2 2.8 collective-permute-done.11
  261.0 2.8 collective-permute-done.5
  263.8 0.0 copy-done
  263.8 0.4 fusion.12
  264.2 0.6 fusion.4
  264.8 0.9 collective-permute-done.2
  265.7 0.4 convolution_bitcast_fusion.1
  266.1 17.8 %fusion = f32[128,16384]{1,0:T(8,128)S(1)} fusion(f32[128,16384]{1,0:T(8,128)} %param.3, f32[2,256,16384]{2,1,0:T(8,128)} %all-gather.2.cloned.1.call-done.v_ref, f32[128,1,256]{2,0,1:T(8,128)S(1)} %bitcast.30, f32[128,1,256]{2,0,1:T(8,128)S(1)} %convolution_bitcast_fusion.1), kind=kOutput, calls=%fused_computation.1 | convolution fusion | flops 6444613632 | bytes 50593792 | tf_op jit(solution)/shard_map/dot_general | solution.py:10
  284.0 96.2 %all_to_all.19 = f32[8,16,16384]{2,1,0:T(8,128)S(1)} all-to-all(f32[8,16,16384]{2,1,0:T(8,128)S(1)} %bitcast.28), channel_id=1, replica_groups=mesh['row'=8,'col'=16] {'row'}, dimensions={0} | all-to-all | bytes 16777216 | tf_op jit(solution)/shard_map/all_to_all | solution.py:98
  380.2 4.0 %copy.7 = f32[8,2,8,16384]{3,2,0,1:T(8,128)} copy(f32[8,2,8,16384]{3,2,1,0:T(8,128)S(1)} %bitcast.27) | data formatting | bytes 16777216 | tf_op jit(solution)/shard_map/all_to_all | solution.py:98
  (6 shorter events, 0.1 us)
Async XLA Ops:
  6.5 191.5 %all-gather.2.cloned.1.call-start = ((), (), s32[]{:S(2)}) async-start(), calls=%async_computation.1 | async-start | bytes 35651584 | tf_op jit(solution)/shard_map/all_gather | solution.py:85
  198.0 65.7 %copy-start = (f32[2,256,256]{2,1,0:T(8,128)S(1)}, f32[2,256,256]{2,1,0:T(8,128)}, u32[]{:S(2)}) copy-start(f32[2,256,256]{2,1,0:T(8,128)} %param.5) | copy-start | bytes 1572868
  231.4 6.6 %collective-permute-start.6 = (f32[128,256]{1,0:T(8,128)}, f32[128,256]{1,0:T(8,128)S(1)}, u32[]{:S(2)}, u32[]{:S(2)}) collective-permute-start(f32[128,256]{1,0:T(8,128)} %get-tuple-element.11), channel_id=1, source_target_pairs={{0,16},{16,0},{32,48},{48,32},{64,80},{80,64},{96,112},{112,96},{1... | collective-permute-start | bytes 393224 | tf_op jit(solution)/shard_map/ppermute | solution.py:27
  231.9 8.8 %collective-permute-start.9 = (f32[128,256]{1,0:T(8,128)}, f32[128,256]{1,0:T(8,128)S(1)}, u32[]{:S(2)}, u32[]{:S(2)}) collective-permute-start(f32[128,256]{1,0:T(8,128)} %get-tuple-element.12), channel_id=1, source_target_pairs={{0,16},{16,0},{32,48},{48,32},{64,80},{80,64},{96,112},{112,96},{1... | collective-permute-start | bytes 393224 | tf_op jit(solution)/shard_map/ppermute | solution.py:27
  233.4 10.2 %collective-permute-start.3 = (f32[256,128]{1,0:T(8,128)}, f32[256,128]{1,0:T(8,128)S(1)}, u32[]{:S(2)}, u32[]{:S(2)}) collective-permute-start(f32[256,128]{1,0:T(8,128)} %get-tuple-element.10), channel_id=1, source_target_pairs={{0,16},{16,0},{32,48},{48,32},{64,80},{80,64},{96,112},{112,96},{1... | collective-permute-start | bytes 393224 | tf_op jit(solution)/shard_map/ppermute | solution.py:27
  234.0 12.1 %collective-permute-start = (f32[256,128]{1,0:T(8,128)}, f32[256,128]{1,0:T(8,128)S(1)}, u32[]{:S(2)}, u32[]{:S(2)}) collective-permute-start(f32[256,128]{1,0:T(8,128)} %get-tuple-element.9), channel_id=1, source_target_pairs={{0,16},{16,0},{32,48},{48,32},{64,80},{80,64},{96,112},{112,96},{1... | collective-permute-start | bytes 393224 | tf_op jit(solution)/shard_map/ppermute | solution.py:27
  238.9 9.3 %collective-permute-start.7 = (f32[128,256]{1,0:T(8,128)S(1)}, f32[128,256]{1,0:T(8,128)S(1)}, u32[]{:S(2)}, u32[]{:S(2)}) collective-permute-start(f32[128,256]{1,0:T(8,128)S(1)} %add.42), channel_id=1, source_target_pairs={{0,32},{16,48},{32,0},{48,16},{64,96},{80,112},{96,64},{112,80},{1... | collective-permute-start | bytes 393224 | tf_op jit(solution)/shard_map/ppermute | solution.py:27
  241.7 9.2 %collective-permute-start.10 = (f32[128,256]{1,0:T(8,128)S(1)}, f32[128,256]{1,0:T(8,128)S(1)}, u32[]{:S(2)}, u32[]{:S(2)}) collective-permute-start(f32[128,256]{1,0:T(8,128)S(1)} %add.45), channel_id=1, source_target_pairs={{0,32},{16,48},{32,0},{48,16},{64,96},{80,112},{96,64},{112,80},{1... | collective-permute-start | bytes 393224 | tf_op jit(solution)/shard_map/ppermute | solution.py:27
  244.5 7.4 %collective-permute-start.4 = (f32[256,128]{1,0:T(8,128)S(1)}, f32[256,128]{1,0:T(8,128)S(1)}, u32[]{:S(2)}, u32[]{:S(2)}) collective-permute-start(f32[256,128]{1,0:T(8,128)S(1)} %add.39), channel_id=1, source_target_pairs={{0,32},{16,48},{32,0},{48,16},{64,96},{80,112},{96,64},{112,80},{1... | collective-permute-start | bytes 393224 | tf_op jit(solution)/shard_map/ppermute | solution.py:27
  247.0 7.7 %collective-permute-start.1 = (f32[256,128]{1,0:T(8,128)S(1)}, f32[256,128]{1,0:T(8,128)S(1)}, u32[]{:S(2)}, u32[]{:S(2)}) collective-permute-start(f32[256,128]{1,0:T(8,128)S(1)} %add.36), channel_id=1, source_target_pairs={{0,32},{16,48},{32,0},{48,16},{64,96},{80,112},{96,64},{112,80},{1... | collective-permute-start | bytes 393224 | tf_op jit(solution)/shard_map/ppermute | solution.py:27
  248.1 10.0 %collective-permute-start.8 = (f32[128,256]{1,0:T(8,128)S(1)}, f32[128,256]{1,0:T(8,128)S(1)}, u32[]{:S(2)}, u32[]{:S(2)}) collective-permute-start(f32[128,256]{1,0:T(8,128)S(1)} %add.43), channel_id=1, source_target_pairs={{0,64},{16,80},{32,96},{48,112},{64,0},{80,16},{96,32},{112,48},{1... | collective-permute-start | bytes 393224 | tf_op jit(solution)/shard_map/ppermute | solution.py:27
  250.9 10.0 %collective-permute-start.11 = (f32[128,256]{1,0:T(8,128)S(1)}, f32[128,256]{1,0:T(8,128)S(1)}, u32[]{:S(2)}, u32[]{:S(2)}) collective-permute-start(f32[128,256]{1,0:T(8,128)S(1)} %add.46), channel_id=1, source_target_pairs={{0,64},{16,80},{32,96},{48,112},{64,0},{80,16},{96,32},{112,48},{1... | collective-permute-start | bytes 393224 | tf_op jit(solution)/shard_map/ppermute | solution.py:27
  251.9 11.9 %collective-permute-start.5 = (f32[256,128]{1,0:T(8,128)S(1)}, f32[256,128]{1,0:T(8,128)S(1)}, u32[]{:S(2)}, u32[]{:S(2)}) collective-permute-start(f32[256,128]{1,0:T(8,128)S(1)} %add.40), channel_id=1, source_target_pairs={{0,64},{16,80},{32,96},{48,112},{64,0},{80,16},{96,32},{112,48},{1... | collective-permute-start | bytes 393224 | tf_op jit(solution)/shard_map/ppermute | solution.py:27
  254.7 11.0 %collective-permute-start.2 = (f32[256,128]{1,0:T(8,128)S(1)}, f32[256,128]{1,0:T(8,128)S(1)}, u32[]{:S(2)}, u32[]{:S(2)}) collective-permute-start(f32[256,128]{1,0:T(8,128)S(1)} %add.37), channel_id=1, source_target_pairs={{0,64},{16,80},{32,96},{48,112},{64,0},{80,16},{96,32},{112,48},{1... | collective-permute-start | bytes 393224 | tf_op jit(solution)/shard_map/ppermute | solution.py:27
Sparse Core Ops, SparseCore 0:
  9.9 188.1 all-gather.1

commit v12 on v10

--- a/solution.py
+++ b/solution.py
@@ -44,16 +44,17 @@
     return lax.dot_general(a, b, (((1,), (0,)), ((), ())), preferred_element_type=jnp.float32)
 
 
-def _proj_kernel(et_hi_ref, et_lo_ref, v_ref, pt_ref, gram_ref):
+def _proj_kernel(et_hi_ref, et_lo_ref, v_ref, outer_ref, inner_ref, gram_ref):
     @pl.when(pl.program_id(0) == 0)
     def _():
-        pt_ref[...] = jnp.zeros_like(pt_ref)
+        outer_ref[...] = jnp.zeros_like(outer_ref)
+        inner_ref[...] = jnp.zeros_like(inner_ref)
         gram_ref[...] = jnp.zeros_like(gram_ref)
     et = (et_hi_ref[...], et_lo_ref[...])
     outer = _split(v_ref[0])
     inner = _split(v_ref[1])
-    pt_ref[0] += _dot_nn(outer[0], et[0]) + _dot_nn(outer[0], et[1]) + _dot_nn(outer[1], et[0])
-    pt_ref[1] += _dot_nn(inner[0], et[0]) + _dot_nn(inner[0], et[1]) + _dot_nn(inner[1], et[0])
+    outer_ref[...] += _dot_nn(outer[0], et[0]) + _dot_nn(outer[0], et[1]) + _dot_nn(outer[1], et[0])
+    inner_ref[...] += _dot_nn(inner[0], et[0]) + _dot_nn(inner[0], et[1]) + _dot_nn(inner[1], et[0])
     gram_ref[...] += _dot3(inner, outer)
 
 
@@ -69,9 +70,11 @@
         in_specs=[pl.BlockSpec((tile, n), lambda i: (i, 0)),
                   pl.BlockSpec((tile, n), lambda i: (i, 0)),
                   pl.BlockSpec((2, k, tile), lambda i: (0, 0, i))],
-        out_specs=[pl.BlockSpec((2, k, n), lambda i: (0, 0, 0)),
+        out_specs=[pl.BlockSpec((k, n), lambda i: (0, 0)),
+                   pl.BlockSpec((k, n), lambda i: (0, 0)),
                    pl.BlockSpec((k, k), lambda i: (0, 0))],
-        out_shape=[jax.ShapeDtypeStruct((2, k, n), jnp.float32),
+        out_shape=[jax.ShapeDtypeStruct((k, n), jnp.float32),
+                   jax.ShapeDtypeStruct((k, n), jnp.float32),
                    jax.ShapeDtypeStruct((k, k), jnp.float32)],
         compiler_params=pltpu.CompilerParams(dimension_semantics=("arbitrary",)),
     )(et_hi, et_lo, panel_t)
@@ -82,9 +85,9 @@
     n = eigvecs.shape[0]
     k = panel.shape[1]
     rows = lax.axis_size("row")
-    proj_t, gram = butterfly_sum(project(eigvecs, panel, 2048), "row", rows)
-    proj_inner = proj_t[1].T
-    proj_outer = proj_t[0].T
+    outer_t, inner_t, gram = butterfly_sum(project(eigvecs, panel, 2048), "row", rows)
+    proj_inner = inner_t.T
+    proj_outer = outer_t.T
     reflected_inner = full_product(proj_inner, coupling[1], ((1,), (1,)))
     proj_outer = proj_outer - full_product(reflected_inner, gram, ((1,), (0,)))
     reflected_outer = full_product(proj_outer, coupling[0], ((1,), (1,)))

time: 384 us -> 383 us (level)
    ppermute x6 -> x9, waiting for transfers between devices: 22.5 us -> 19.9 us  [butterfly_sum(): x = jax.tree_util.tree_map(jnp.add, x, lax.ppermute(x, axis, pairs))]
    ppermute x6 -> x9, starting transfers between devices: 11.3 us -> 12.5 us  [butterfly_sum(): x = jax.tree_util.tree_map(jnp.add, x, lax.ppermute(x, axis, pairs))]
  transfers between devices with their start and end apart: 7 -> 10, of which waited for: 7 -> 7; matrix products, arithmetic and copies ran while one was open for 5% -> 5% of each run, Pallas kernels for 0% -> 0%
where the time goes in v12:
time: 383 us
  waiting for transfers between devices  196 us (51%)
  blocking collectives  94.8 us (25%)
  Pallas kernels  24.6 us (6%)
  matrix products  19.2 us (5%)
  between operations  13.4 us (3%)
  local copies, waits for them, and re-layouts  13 us (3%)
  starting transfers between devices  12.5 us (3%)
  other arithmetic  9.14 us (2%)
    all_gather x1, waiting for transfers between devices, body(): panel = lax.all_gather(jnp.swapaxes(basis, 1, 2), 'col', axis=1, tiled=True)  176 us
    all_to_all x1, blocking collectives, body(): lax.all_to_all(current, 'row', split_axis=0, concat_axis=1, tiled=True)  94.8 us
    pallas_call x1, Pallas kernels, project(): pl.pallas_call(_proj_kernel, grid=(m // tile,), in_specs=[pl.BlockSpec((t...  24.6 us
    ppermute x9, waiting for transfers between devices, butterfly_sum(): x = jax.tree_util.tree_map(jnp.add, x, lax.ppermute(x, axis, pairs))  19.9 us
    dot_general x4, matrix products, full_product(): lax.dot_general(former, latter, (contract_dims, ((), ())), precision=prec...  19.2 us
    ppermute x9, starting transfers between devices, butterfly_sum(): x = jax.tree_util.tree_map(jnp.add, x, lax.ppermute(x, axis, pairs))  12.5 us
    unnamed x3, local copies, waits for them, and re-layouts  8.99 us
  transfers between devices with their start and end apart: 10, of which 7 were waited for; matrix products, arithmetic and copies ran while one was open for 5% of the time, Pallas kernels for 0%

profile of v12, /device:TPU:0, one launch (start us, length us, event | category | flops | bytes accessed | tf_op | source)
XLA Modules:
  0.0 382.8 jit_solution(17701491456141176781)
XLA Ops:
  6.5 0.0 all-gather.2.cloned.1.call-start
  6.5 0.7 all-gather.2.cloned.1.call-update
  7.3 9.0 %copy.4 = f32[128,16384]{0,1:T(8,128)} copy(f32[128,16384]{1,0:T(8,128)} %param.3) | data formatting | bytes 16777216 | tf_op args[0]
  16.2 6.2 %fusion.2 = (bf16[16384,128]{1,0:T(8,128)(2,1)}, bf16[16384,128]{1,0:T(8,128)(2,1)}) fusion(f32[128,16384]{0,1:T(8,128)} %copy.4), kind=kLoop, calls=%fused_computation.5 | loop fusion | flops 8388608 | bytes 16777216 | tf_op jit(solution)/shard_map/convert_element_type | solution.py:66
  22.5 175.6 %all-gather.2.cloned.1.call-done.v_ref = f32[2,256,16384]{2,1,0:T(8,128)} async-done(((f32[2,16,16384]{2,1,0:T(8,128)}), f32[2,256,16384]{2,1,0:T(8,128)}) %all-gather.2.cloned.1.call-update) | async-done | bytes 33554448 | tf_op jit(solution)/shard_map/all_gather | solution.py:84
  198.0 0.0 copy-start
  198.0 24.6 %shard_map.37 = (f32[256,128]{1,0:T(8,128)}, f32[256,128]{1,0:T(8,128)}, f32[256,256]{1,0:T(8,128)}) custom-call(bf16[16384,128]{1,0:T(8,128)(2,1)} %get-tuple-element.12.et_hi_ref, bf16[16384,128]{1,0:T(8,128)(2,1)} %get-tuple-element.11.et_lo_ref, f32[2,256,16384]{2,1,0:T(8,128)} %all-gather.2.cloned.1.call-done.v_ref), custom_call_target="tpu_custom_call" | custom-call | tf_op jit(solution)/shard_map/pallas_call | solution.py:67
  222.6 0.6 collective-permute-start.6
  223.2 1.5 collective-permute-start.3
  224.7 7.4 %collective-permute-done.6 = f32[256,256]{1,0:T(8,128)S(1)} collective-permute-done((f32[256,256]{1,0:T(8,128)}, f32[256,256]{1,0:T(8,128)S(1)}, u32[]{:S(2)}, u32[]{:S(2)}) %collective-permute-start.6) | collective-permute-done | bytes 262176 | tf_op jit(solution)/shard_map/ppermute | solution.py:27
  232.0 1.0 add.33
  233.0 1.6 collective-permute-start.7
  234.6 0.6 collective-permute-start
  235.1 0.0 collective-permute-done.3
  235.1 0.9 add.30
  236.1 0.6 collective-permute-start.4
  236.7 3.0 collective-permute-done
  239.7 0.9 add.27
  240.7 0.6 collective-permute-start.1
  241.3 2.9 collective-permute-done.4
  244.2 3.4 collective-permute-start.5
  247.5 0.0 collective-permute-done.7
  247.6 0.3 collective-permute-start.8
  247.9 0.0 collective-permute-done.1
  247.9 3.4 collective-permute-start.2
  251.3 1.5 collective-permute-done.5
  252.8 0.0 copy-done
  252.8 0.4 fusion.8
  253.2 4.3 %collective-permute-done.8 = f32[256,256]{1,0:T(8,128)S(1)} collective-permute-done((f32[256,256]{1,0:T(8,128)S(1)}, f32[256,256]{1,0:T(8,128)S(1)}, u32[]{:S(2)}, u32[]{:S(2)}) %collective-permute-start.8) | collective-permute-done | bytes 262176 | tf_op jit(solution)/shard_map/ppermute | solution.py:27
  257.5 0.6 fusion.11
  258.1 0.8 collective-permute-done.2
  258.9 0.4 convolution_bitcast_fusion.1
  259.4 17.8 %fusion = f32[128,16384]{1,0:T(8,128)S(1)} fusion(f32[128,16384]{1,0:T(8,128)} %param.3, f32[2,256,16384]{2,1,0:T(8,128)} %all-gather.2.cloned.1.call-done.v_ref, f32[128,1,256]{2,0,1:T(8,128)S(1)} %bitcast.30, f32[128,1,256]{2,0,1:T(8,128)S(1)} %convolution_bitcast_fusion.1), kind=kOutput, calls=%fused_computation.1 | convolution fusion | flops 6444613632 | bytes 50593792 | tf_op jit(solution)/shard_map/dot_general | solution.py:10
  277.2 94.8 %all_to_all.19 = f32[8,16,16384]{2,1,0:T(8,128)S(1)} all-to-all(f32[8,16,16384]{2,1,0:T(8,128)S(1)} %bitcast.28), channel_id=1, replica_groups=mesh['row'=8,'col'=16] {'row'}, dimensions={0} | all-to-all | bytes 16777216 | tf_op jit(solution)/shard_map/all_to_all | solution.py:96
  372.0 4.0 %copy.7 = f32[8,2,8,16384]{3,2,0,1:T(8,128)} copy(f32[8,2,8,16384]{3,2,1,0:T(8,128)S(1)} %bitcast.27) | data formatting | bytes 16777216 | tf_op jit(solution)/shard_map/all_to_all | solution.py:96
  (3 shorter events, 0.1 us)
Async XLA Ops:
  6.5 191.5 %all-gather.2.cloned.1.call-start = ((), (), s32[]{:S(2)}) async-start(), calls=%async_computation.1 | async-start | bytes 35651584 | tf_op jit(solution)/shard_map/all_gather | solution.py:84
  198.0 54.8 %copy-start = (f32[2,256,256]{2,1,0:T(8,128)S(1)}, f32[2,256,256]{2,1,0:T(8,128)}, u32[]{:S(2)}) copy-start(f32[2,256,256]{2,1,0:T(8,128)} %param.5) | copy-start | bytes 1572868
  222.6 9.4 %collective-permute-start.6 = (f32[256,256]{1,0:T(8,128)}, f32[256,256]{1,0:T(8,128)S(1)}, u32[]{:S(2)}, u32[]{:S(2)}) collective-permute-start(f32[256,256]{1,0:T(8,128)} %get-tuple-element.10), channel_id=1, source_target_pairs={{0,16},{16,0},{32,48},{48,32},{64,80},{80,64},{96,112},{112,96},{1... | collective-permute-start | bytes 786440 | tf_op jit(solution)/shard_map/ppermute | solution.py:27
  223.2 11.9 %collective-permute-start.3 = (f32[256,128]{1,0:T(8,128)}, f32[256,128]{1,0:T(8,128)S(1)}, u32[]{:S(2)}, u32[]{:S(2)}) collective-permute-start(f32[256,128]{1,0:T(8,128)} %get-tuple-element.9), channel_id=1, source_target_pairs={{0,16},{16,0},{32,48},{48,32},{64,80},{80,64},{96,112},{112,96},{1... | collective-permute-start | bytes 393224 | tf_op jit(solution)/shard_map/ppermute | solution.py:27
  233.0 14.5 %collective-permute-start.7 = (f32[256,256]{1,0:T(8,128)S(1)}, f32[256,256]{1,0:T(8,128)S(1)}, u32[]{:S(2)}, u32[]{:S(2)}) collective-permute-start(f32[256,256]{1,0:T(8,128)S(1)} %add.33), channel_id=1, source_target_pairs={{0,32},{16,48},{32,0},{48,16},{64,96},{80,112},{96,64},{112,80},{1... | collective-permute-start | bytes 786440 | tf_op jit(solution)/shard_map/ppermute | solution.py:27
  234.6 5.2 %collective-permute-start = (f32[256,128]{1,0:T(8,128)}, f32[256,128]{1,0:T(8,128)S(1)}, u32[]{:S(2)}, u32[]{:S(2)}) collective-permute-start(f32[256,128]{1,0:T(8,128)} %get-tuple-element.8), channel_id=1, source_target_pairs={{0,16},{16,0},{32,48},{48,32},{64,80},{80,64},{96,112},{112,96},{1... | collective-permute-start | bytes 393224 | tf_op jit(solution)/shard_map/ppermute | solution.py:27
  236.1 8.1 %collective-permute-start.4 = (f32[256,128]{1,0:T(8,128)S(1)}, f32[256,128]{1,0:T(8,128)S(1)}, u32[]{:S(2)}, u32[]{:S(2)}) collective-permute-start(f32[256,128]{1,0:T(8,128)S(1)} %add.30), channel_id=1, source_target_pairs={{0,32},{16,48},{32,0},{48,16},{64,96},{80,112},{96,64},{112,80},{1... | collective-permute-start | bytes 393224 | tf_op jit(solution)/shard_map/ppermute | solution.py:27
  240.7 7.2 %collective-permute-start.1 = (f32[256,128]{1,0:T(8,128)S(1)}, f32[256,128]{1,0:T(8,128)S(1)}, u32[]{:S(2)}, u32[]{:S(2)}) collective-permute-start(f32[256,128]{1,0:T(8,128)S(1)} %add.27), channel_id=1, source_target_pairs={{0,32},{16,48},{32,0},{48,16},{64,96},{80,112},{96,64},{112,80},{1... | collective-permute-start | bytes 393224 | tf_op jit(solution)/shard_map/ppermute | solution.py:27
  244.2 8.6 %collective-permute-start.5 = (f32[256,128]{1,0:T(8,128)S(1)}, f32[256,128]{1,0:T(8,128)S(1)}, u32[]{:S(2)}, u32[]{:S(2)}) collective-permute-start(f32[256,128]{1,0:T(8,128)S(1)} %add.31), channel_id=1, source_target_pairs={{0,64},{16,80},{32,96},{48,112},{64,0},{80,16},{96,32},{112,48},{1... | collective-permute-start | bytes 393224 | tf_op jit(solution)/shard_map/ppermute | solution.py:27
  247.6 10.0 %collective-permute-start.8 = (f32[256,256]{1,0:T(8,128)S(1)}, f32[256,256]{1,0:T(8,128)S(1)}, u32[]{:S(2)}, u32[]{:S(2)}) collective-permute-start(f32[256,256]{1,0:T(8,128)S(1)} %add.34), channel_id=1, source_target_pairs={{0,64},{16,80},{32,96},{48,112},{64,0},{80,16},{96,32},{112,48},{1... | collective-permute-start | bytes 786440 | tf_op jit(solution)/shard_map/ppermute | solution.py:27
  247.9 11.0 %collective-permute-start.2 = (f32[256,128]{1,0:T(8,128)S(1)}, f32[256,128]{1,0:T(8,128)S(1)}, u32[]{:S(2)}, u32[]{:S(2)}) collective-permute-start(f32[256,128]{1,0:T(8,128)S(1)} %add.28), channel_id=1, source_target_pairs={{0,64},{16,80},{32,96},{48,112},{64,0},{80,16},{96,32},{112,48},{1... | collective-permute-start | bytes 393224 | tf_op jit(solution)/shard_map/ppermute | solution.py:27
Sparse Core Ops, SparseCore 0:
  9.9 188.1 all-gather.1

commit v13 on v12

--- a/solution.py
+++ b/solution.py
@@ -88,9 +88,9 @@
     outer_t, inner_t, gram = butterfly_sum(project(eigvecs, panel, 2048), "row", rows)
     proj_inner = inner_t.T
     proj_outer = outer_t.T
-    reflected_inner = full_product(proj_inner, coupling[1], ((1,), (1,)))
-    proj_outer = proj_outer - full_product(reflected_inner, gram, ((1,), (0,)))
-    reflected_outer = full_product(proj_outer, coupling[0], ((1,), (1,)))
+    reflected_inner = large_product(proj_inner, coupling[1], ((1,), (1,)))
+    proj_outer = proj_outer - large_product(reflected_inner, gram, ((1,), (0,)))
+    reflected_outer = large_product(proj_outer, coupling[0], ((1,), (1,)))
     reflected = jnp.stack([reflected_outer, reflected_inner], axis=1)
     current = eigvecs - large_product(reflected, panel, ((1, 2), (0, 1)))
     return lax.all_to_all(current, "row", split_axis=0, concat_axis=1, tiled=True)

time: 383 us -> 383 us (level)
  no operation moved by 1% of the time
where the time goes in v13:
time: 383 us
  waiting for transfers between devices  196 us (51%)
  blocking collectives  94.8 us (25%)
  Pallas kernels  24.6 us (6%)
  matrix products  18.8 us (5%)
  between operations  13.4 us (3%)
  local copies, waits for them, and re-layouts  13 us (3%)
  starting transfers between devices  12.5 us (3%)
  other arithmetic  9.14 us (2%)
    all_gather x1, waiting for transfers between devices, body(): panel = lax.all_gather(jnp.swapaxes(basis, 1, 2), 'col', axis=1, tiled=True)  176 us
    all_to_all x1, blocking collectives, body(): lax.all_to_all(current, 'row', split_axis=0, concat_axis=1, tiled=True)  94.8 us
    pallas_call x1, Pallas kernels, project(): pl.pallas_call(_proj_kernel, grid=(m // tile,), in_specs=[pl.BlockSpec((t...  24.6 us
    ppermute x9, waiting for transfers between devices, butterfly_sum(): x = jax.tree_util.tree_map(jnp.add, x, lax.ppermute(x, axis, pairs))  20.2 us
    dot_general x4, matrix products, full_product(): lax.dot_general(former, latter, (contract_dims, ((), ())), precision=prec...  18.8 us
    ppermute x9, starting transfers between devices, butterfly_sum(): x = jax.tree_util.tree_map(jnp.add, x, lax.ppermute(x, axis, pairs))  12.5 us
    unnamed x3, local copies, waits for them, and re-layouts  8.99 us
  transfers between devices with their start and end apart: 10, of which 7 were waited for; matrix products, arithmetic and copies ran while one was open for 5% of the time, Pallas kernels for 0%

profile of v13, /device:TPU:0, one launch (start us, length us, event | category | flops | bytes accessed | tf_op | source)
XLA Modules:
  0.0 382.8 jit_solution(3703865215013752674)
XLA Ops:
  6.5 0.0 all-gather.2.cloned.1.call-start
  6.5 0.7 all-gather.2.cloned.1.call-update
  7.3 9.0 %copy.4 = f32[128,16384]{0,1:T(8,128)} copy(f32[128,16384]{1,0:T(8,128)} %param.3) | data formatting | bytes 16777216 | tf_op args[0]
  16.2 6.2 %fusion.2 = (bf16[16384,128]{1,0:T(8,128)(2,1)}, bf16[16384,128]{1,0:T(8,128)(2,1)}) fusion(f32[128,16384]{0,1:T(8,128)} %copy.4), kind=kLoop, calls=%fused_computation.5 | loop fusion | flops 8388608 | bytes 16777216 | tf_op jit(solution)/shard_map/convert_element_type | solution.py:66
  22.5 175.6 %all-gather.2.cloned.1.call-done.v_ref = f32[2,256,16384]{2,1,0:T(8,128)} async-done(((f32[2,16,16384]{2,1,0:T(8,128)}), f32[2,256,16384]{2,1,0:T(8,128)}) %all-gather.2.cloned.1.call-update) | async-done | bytes 33554448 | tf_op jit(solution)/shard_map/all_gather | solution.py:84
  198.0 0.0 copy-start
  198.0 24.6 %shard_map.37 = (f32[256,128]{1,0:T(8,128)}, f32[256,128]{1,0:T(8,128)}, f32[256,256]{1,0:T(8,128)}) custom-call(bf16[16384,128]{1,0:T(8,128)(2,1)} %get-tuple-element.12.et_hi_ref, bf16[16384,128]{1,0:T(8,128)(2,1)} %get-tuple-element.11.et_lo_ref, f32[2,256,16384]{2,1,0:T(8,128)} %all-gather.2.cloned.1.call-done.v_ref), custom_call_target="tpu_custom_call" | custom-call | tf_op jit(solution)/shard_map/pallas_call | solution.py:67
  222.6 0.6 collective-permute-start.6
  223.2 1.5 collective-permute-start.3
  224.7 7.4 %collective-permute-done.6 = f32[256,256]{1,0:T(8,128)S(1)} collective-permute-done((f32[256,256]{1,0:T(8,128)}, f32[256,256]{1,0:T(8,128)S(1)}, u32[]{:S(2)}, u32[]{:S(2)}) %collective-permute-start.6) | collective-permute-done | bytes 262176 | tf_op jit(solution)/shard_map/ppermute | solution.py:27
  232.0 1.0 add.33
  233.0 1.6 collective-permute-start.7
  234.6 0.6 collective-permute-start
  235.1 0.0 collective-permute-done.3
  235.1 0.9 add.30
  236.1 0.6 collective-permute-start.4
  236.7 3.0 collective-permute-done
  239.7 0.9 add.27
  240.7 0.6 collective-permute-start.1
  241.3 2.9 collective-permute-done.4
  244.2 3.4 collective-permute-start.5
  247.5 0.0 collective-permute-done.7
  247.6 0.3 collective-permute-start.8
  247.9 0.0 collective-permute-done.1
  247.9 3.4 collective-permute-start.2
  251.3 1.5 collective-permute-done.5
  252.8 0.0 copy-done
  252.8 0.3 fusion.8
  253.1 4.4 %collective-permute-done.8 = f32[256,256]{1,0:T(8,128)S(1)} collective-permute-done((f32[256,256]{1,0:T(8,128)S(1)}, f32[256,256]{1,0:T(8,128)S(1)}, u32[]{:S(2)}, u32[]{:S(2)}) %collective-permute-start.8) | collective-permute-done | bytes 262176 | tf_op jit(solution)/shard_map/ppermute | solution.py:27
  257.5 0.4 fusion.11
  257.9 1.0 collective-permute-done.2
  258.9 0.3 convolution_bitcast_fusion.1
  259.3 17.8 %fusion = f32[128,16384]{1,0:T(8,128)S(1)} fusion(f32[128,16384]{1,0:T(8,128)} %param.3, f32[2,256,16384]{2,1,0:T(8,128)} %all-gather.2.cloned.1.call-done.v_ref, f32[128,1,256]{2,0,1:T(8,128)S(1)} %bitcast.30, f32[128,1,256]{2,0,1:T(8,128)S(1)} %convolution_bitcast_fusion.1), kind=kOutput, calls=%fused_computation.1 | convolution fusion | flops 6444613632 | bytes 50593792 | tf_op jit(solution)/shard_map/dot_general | solution.py:10
  277.1 94.8 %all_to_all.19 = f32[8,16,16384]{2,1,0:T(8,128)S(1)} all-to-all(f32[8,16,16384]{2,1,0:T(8,128)S(1)} %bitcast.28), channel_id=1, replica_groups=mesh['row'=8,'col'=16] {'row'}, dimensions={0} | all-to-all | bytes 16777216 | tf_op jit(solution)/shard_map/all_to_all | solution.py:96
  371.9 4.0 %copy.7 = f32[8,2,8,16384]{3,2,0,1:T(8,128)} copy(f32[8,2,8,16384]{3,2,1,0:T(8,128)S(1)} %bitcast.27) | data formatting | bytes 16777216 | tf_op jit(solution)/shard_map/all_to_all | solution.py:96
  (3 shorter events, 0.1 us)
Async XLA Ops:
  6.5 191.5 %all-gather.2.cloned.1.call-start = ((), (), s32[]{:S(2)}) async-start(), calls=%async_computation.1 | async-start | bytes 35651584 | tf_op jit(solution)/shard_map/all_gather | solution.py:84
  198.0 54.8 %copy-start = (f32[2,256,256]{2,1,0:T(8,128)S(1)}, f32[2,256,256]{2,1,0:T(8,128)}, u32[]{:S(2)}) copy-start(f32[2,256,256]{2,1,0:T(8,128)} %param.5) | copy-start | bytes 1572868
  222.6 9.4 %collective-permute-start.6 = (f32[256,256]{1,0:T(8,128)}, f32[256,256]{1,0:T(8,128)S(1)}, u32[]{:S(2)}, u32[]{:S(2)}) collective-permute-start(f32[256,256]{1,0:T(8,128)} %get-tuple-element.10), channel_id=1, source_target_pairs={{0,16},{16,0},{32,48},{48,32},{64,80},{80,64},{96,112},{112,96},{1... | collective-permute-start | bytes 786440 | tf_op jit(solution)/shard_map/ppermute | solution.py:27
  223.2 11.9 %collective-permute-start.3 = (f32[256,128]{1,0:T(8,128)}, f32[256,128]{1,0:T(8,128)S(1)}, u32[]{:S(2)}, u32[]{:S(2)}) collective-permute-start(f32[256,128]{1,0:T(8,128)} %get-tuple-element.9), channel_id=1, source_target_pairs={{0,16},{16,0},{32,48},{48,32},{64,80},{80,64},{96,112},{112,96},{1... | collective-permute-start | bytes 393224 | tf_op jit(solution)/shard_map/ppermute | solution.py:27
  233.0 14.5 %collective-permute-start.7 = (f32[256,256]{1,0:T(8,128)S(1)}, f32[256,256]{1,0:T(8,128)S(1)}, u32[]{:S(2)}, u32[]{:S(2)}) collective-permute-start(f32[256,256]{1,0:T(8,128)S(1)} %add.33), channel_id=1, source_target_pairs={{0,32},{16,48},{32,0},{48,16},{64,96},{80,112},{96,64},{112,80},{1... | collective-permute-start | bytes 786440 | tf_op jit(solution)/shard_map/ppermute | solution.py:27
  234.6 5.2 %collective-permute-start = (f32[256,128]{1,0:T(8,128)}, f32[256,128]{1,0:T(8,128)S(1)}, u32[]{:S(2)}, u32[]{:S(2)}) collective-permute-start(f32[256,128]{1,0:T(8,128)} %get-tuple-element.8), channel_id=1, source_target_pairs={{0,16},{16,0},{32,48},{48,32},{64,80},{80,64},{96,112},{112,96},{1... | collective-permute-start | bytes 393224 | tf_op jit(solution)/shard_map/ppermute | solution.py:27
  236.1 8.1 %collective-permute-start.4 = (f32[256,128]{1,0:T(8,128)S(1)}, f32[256,128]{1,0:T(8,128)S(1)}, u32[]{:S(2)}, u32[]{:S(2)}) collective-permute-start(f32[256,128]{1,0:T(8,128)S(1)} %add.30), channel_id=1, source_target_pairs={{0,32},{16,48},{32,0},{48,16},{64,96},{80,112},{96,64},{112,80},{1... | collective-permute-start | bytes 393224 | tf_op jit(solution)/shard_map/ppermute | solution.py:27
  240.7 7.2 %collective-permute-start.1 = (f32[256,128]{1,0:T(8,128)S(1)}, f32[256,128]{1,0:T(8,128)S(1)}, u32[]{:S(2)}, u32[]{:S(2)}) collective-permute-start(f32[256,128]{1,0:T(8,128)S(1)} %add.27), channel_id=1, source_target_pairs={{0,32},{16,48},{32,0},{48,16},{64,96},{80,112},{96,64},{112,80},{1... | collective-permute-start | bytes 393224 | tf_op jit(solution)/shard_map/ppermute | solution.py:27
  244.2 8.6 %collective-permute-start.5 = (f32[256,128]{1,0:T(8,128)S(1)}, f32[256,128]{1,0:T(8,128)S(1)}, u32[]{:S(2)}, u32[]{:S(2)}) collective-permute-start(f32[256,128]{1,0:T(8,128)S(1)} %add.31), channel_id=1, source_target_pairs={{0,64},{16,80},{32,96},{48,112},{64,0},{80,16},{96,32},{112,48},{1... | collective-permute-start | bytes 393224 | tf_op jit(solution)/shard_map/ppermute | solution.py:27
  247.6 10.0 %collective-permute-start.8 = (f32[256,256]{1,0:T(8,128)S(1)}, f32[256,256]{1,0:T(8,128)S(1)}, u32[]{:S(2)}, u32[]{:S(2)}) collective-permute-start(f32[256,256]{1,0:T(8,128)S(1)} %add.34), channel_id=1, source_target_pairs={{0,64},{16,80},{32,96},{48,112},{64,0},{80,16},{96,32},{112,48},{1... | collective-permute-start | bytes 786440 | tf_op jit(solution)/shard_map/ppermute | solution.py:27
  247.9 11.0 %collective-permute-start.2 = (f32[256,128]{1,0:T(8,128)S(1)}, f32[256,128]{1,0:T(8,128)S(1)}, u32[]{:S(2)}, u32[]{:S(2)}) collective-permute-start(f32[256,128]{1,0:T(8,128)S(1)} %add.28), channel_id=1, source_target_pairs={{0,64},{16,80},{32,96},{48,112},{64,0},{80,16},{96,32},{112,48},{1... | collective-permute-start | bytes 393224 | tf_op jit(solution)/shard_map/ppermute | solution.py:27
Sparse Core Ops, SparseCore 0:
  9.9 188.1 all-gather.1
